TPU v7x, 32 devices: a whole 2x2x4 slice. The times are simulated.
32 devices in a mesh: groups: 2 (over x), energy: 8 (over z, y), space: 2 (over core).
Axes of the slice: x: 2, y: 2, z: 4, core: 2. Of those that a mesh axis runs over, the one named last changes fastest.
Arguments:
- ham_diag: float32 [2, 2, 512, 256], P('space', None, 'groups'), parts along dimension 2, as said below
- ham_coupling: float32 [2, 2, 256, 256], P('groups'), parts along dimension 0, may hold values from -0.25 to 0.25
- sigma_shift: float32 [8, 2, 512], P('energy', 'space', 'groups'), parts along dimension 2, may hold values from -3 to 3
- sigma_width: float32 [8, 2, 512], P('energy', 'space', 'groups'), parts along dimension 2, may hold values from 0.5 to 2
- occupation: float32 [8, 2, 512], P('energy', 'space', 'groups'), parts along dimension 2, may hold values from 0 to 1
Outputs:
- polarization: float32 [16, 2, 2, 256, 256], P('groups', None, None, ('energy', 'space')), parts along dimension 0
There are 2 independent parts, one for each index of `groups`. A program takes and returns all parts, laid end to end along the dimension named above; each array names one. Nothing has to cross between parts.
Inputs may be any that keep to these rules, and one draw needn't show every extreme that they name: Each ham_diag[b, 0] is symmetric and each ham_diag[b, 1] antisymmetric.
All inputs are finite; a program needn't handle non-finite values.
Results may differ from a plain program's by a relative error of at most 0.0001.
Values sent between devices are 32-bit elements; how exact they have to be, the bound alone decides.
No kernel may reach another device: no remote copies, remote signals or barrier semaphores. Data moves between devices by JAX's collectives and lax.ppermute only.
A program may use at most 64 MiB of HBM per device.

v0:
```python
import jax
import jax.numpy as jnp
from jax import lax
from jax.sharding import PartitionSpec as P


def from_partner(shard, axis, distance):
    return lax.ppermute(shard, axis, [(i, i ^ 1 << distance) for i in range(lax.axis_size(axis))])


def dot(left, right, precision=lax.Precision.HIGHEST):
    return jnp.einsum("...ij,...jk->...ik", left, right, precision=precision)


def swap(value):
    return jnp.swapaxes(value, -1, -2)


def embed(real, imag):
    top = jnp.concatenate([real, -imag], axis=-1)
    bottom = jnp.concatenate([imag, real], axis=-1)
    return jnp.concatenate([top, bottom], axis=-2)


def stack(real, imag):
    return jnp.concatenate([real, imag], axis=-2)


def split(stacked):
    order = stacked.shape[-2] // 2
    return stacked[..., :order, :], stacked[..., order:, :]


def stacked_adjoint(real, imag):
    return stack(swap(real), -swap(imag))


def invert(matrix):
    order = matrix.shape[-1] // 2
    eye = stack(jnp.eye(order, dtype=jnp.float32), jnp.zeros((order, order), jnp.float32))
    high = lax.Precision.HIGH
    gram = jnp.einsum("...ij,...kj->...ik", matrix, matrix[..., :order, :], precision=high)
    square = dot(embed(*split(gram)), gram, high)
    fourth = dot(embed(*split(square)), square, high)
    fourth_re, fourth_im = split(fourth)
    rows = jnp.sum(jnp.abs(fourth_re) + jnp.abs(fourth_im), axis=-1)
    beta = jnp.sqrt(jnp.sqrt(jnp.max(rows, axis=-1))) * 1.01 + 1e-30
    beta = beta[..., None, None]
    lower = 0.25 / beta
    alpha = 2.0 / (lower + 1.0)
    first_step = 2.0 * eye - (alpha / beta) * gram
    approx = jnp.einsum("...ji,...jk->...ik", matrix, first_step, precision=high) * (alpha / beta)
    ratio = (1.0 - lower) / (1.0 + lower)
    lower = 1.0 - ratio * ratio
    for _ in range(5):
        alpha = 2.0 / (lower + 1.0)
        product = dot(matrix, approx, high)
        approx = dot(alpha * embed(*split(approx)), 2.0 * eye - alpha * product, high)
        ratio = (1.0 - lower) / (1.0 + lower)
        lower = 1.0 - ratio * ratio

    def keep_going(state):
        _, residual, count = state
        return (residual > 2e-3) & (count < 40)

    def newton(state):
        approx, _, count = state
        rest = eye - dot(matrix, approx)
        residual = jnp.sqrt(jnp.max(jnp.sum(rest * rest, axis=(-1, -2))))
        return approx + dot(embed(*split(approx)), rest, high), residual, count + 1

    approx, _, _ = lax.while_loop(
        keep_going, newton, (approx, jnp.float32(jnp.inf), jnp.int32(0))
    )
    return approx


def body(ham_diag, ham_coupling, sigma_shift, sigma_width, occupation):
    blocks = ham_diag.shape[0]
    assert blocks == 1
    energies_here = sigma_shift.shape[0]
    order = ham_diag.shape[-1]
    side = lax.axis_index("space")
    first = side == 0
    total = energies_here * lax.axis_size("energy")
    offset = lax.axis_index("energy") * energies_here
    energy = -2.0 + 4.0 * ((offset + jnp.arange(energies_here)).astype(jnp.float32) + 0.5) / total
    identity = jnp.eye(order, dtype=jnp.float32)
    shift = sigma_shift[:, 0]
    width = sigma_width[:, 0]
    source = 2.0 * occupation[:, 0] * width
    real_part = (
        energy[:, None, None] * identity
        - ham_diag[None, 0, 0]
        - shift[:, :, None] * identity
    )
    imag_part = width[:, :, None] * identity - ham_diag[None, 0, 1]
    system = embed(real_part, imag_part)

    green_col = invert(system)
    g_re, g_im = split(green_col)
    scaled = embed(-g_im * source[:, None, :], g_re * source[:, None, :])
    link = ham_coupling[0]
    link_re = jnp.where(first, swap(link[0]), link[0])
    link_im = jnp.where(first, -swap(link[1]), link[1])
    link_embed = embed(link_re, link_im)
    link_adj = stacked_adjoint(link_re, link_im)
    high = lax.Precision.HIGH
    left_green = dot(link_embed, green_col, high)
    coupled_green = from_partner(dot(embed(*split(left_green)), link_adj, high), "space", 0)
    green_less = dot(scaled, stacked_adjoint(g_re, g_im), high)
    left_less = dot(link_embed, green_less, high)
    coupled_less = from_partner(dot(embed(*split(left_less)), link_adj, high), "space", 0)

    full_re, full_im = split(invert(system - embed(*split(coupled_green))))
    less_re, less_im = split(coupled_less)
    less_im = less_im + source[:, :, None] * identity
    inner = dot(embed(full_re, full_im), stack(less_re, less_im), high)
    lesser = dot(embed(*split(inner)), stacked_adjoint(full_re, full_im), high)
    lesser_re, lesser_im = split(lesser)
    greater_re = lesser_re + full_re - swap(full_re)
    greater_im = lesser_im + full_im + swap(full_im)

    chunks = lax.axis_size("energy") * lax.axis_size("space")
    row_count = order // chunks
    parts = [lesser_re, lesser_im, greater_re, greater_im]
    parts = [part.reshape((energies_here, chunks, row_count, order)) for part in parts]
    paired = jnp.moveaxis(jnp.stack(parts, axis=2), 1, 0)
    arrived = lax.all_to_all(paired, ("energy", "space"), split_axis=0, concat_axis=0, tiled=True)
    arrived = arrived.reshape(
        (lax.axis_size("energy"), lax.axis_size("space"), energies_here, 4, row_count, order)
    )
    arrived = jnp.transpose(arrived, (0, 2, 1, 3, 4, 5))
    regrouped = arrived.reshape((total, lax.axis_size("space"), 2, 2, row_count, order))
    a_re, a_im = regrouped[:, :, 0, 0], regrouped[:, :, 0, 1]
    b_re, b_im = regrouped[:, :, 1, 0], regrouped[:, :, 1, 1]
    corr_re = []
    corr_im = []
    for shift_index in range(total):
        upper_re, upper_im = a_re[shift_index:], a_im[shift_index:]
        lower_re, lower_im = b_re[: total - shift_index], b_im[: total - shift_index]
        corr_re.append(jnp.sum(upper_re * lower_re + upper_im * lower_im, axis=0))
        corr_im.append(jnp.sum(upper_im * lower_re - upper_re * lower_im, axis=0))
    corr_re = jnp.stack(corr_re, axis=0)
    corr_im = jnp.stack(corr_im, axis=0)
    return jnp.stack([-order * corr_im, order * corr_re], axis=2)


def solution(mesh):
    return jax.shard_map(
        body,
        mesh=mesh,
        in_specs=(
            P("space", None, "groups", None),
            P("groups", None, None, None),
            P("energy", "space", "groups"),
            P("energy", "space", "groups"),
            P("energy", "space", "groups"),
        ),
        out_specs=P("groups", None, None, ("energy", "space"), None),
        check_vma=False,
    )
```

profile of v0, /device:TPU:1, one launch (start us, length us, event | category | flops | bytes accessed | tf_op | source)
XLA Modules:
  0.0 80.6 jit_solution(6553412028306350052)
XLA Ops:
  0.1 0.7 copy-done.3
  0.7 1.2 %fusion.177 = (f32[1,256,256]{2,1,0:T(8,128)S(1)}, f32[1,256,256]{2,1,0:T(8,128)S(1)}, f32[1,256,256]{2,1,0:T(8,128)S(1)}) fusion(f32[1,2,256,256]{3,2,1,0:T(8,128)} %param.9, f32[256]{0:T(256)S(1)} %bitcast.390, f32[256]{0:T(256)S(1)} %bitcast.394, f32[]{:T(128)S(6)} %add.151), kind=kLoop, calls=%fused_computation.353 | loop fusion | flops 524288 | bytes 1312772 | tf_op jit(solution)/shard_map/neg | solution.py:20
  5.8 0.6 convolution_multiply_fusion.11
  12.2 0.8 slice_negate_fusion.14
  13.0 1.4 %select_subtract_fusion.6 = f32[512,256]{0,1:T(8,128)} fusion(f32[512,256]{0,1:T(8,128)S(1)} %fusion.42, pred[256,256]{0,1:T(32,128)(4,1)S(1)} %iota_compare_fusion, f32[]{:T(128)} %bitcast.21, f32[1,256,256]{2,1,0:T(8,128)S(1)} %get-tuple-element.215, f32[1,256,256]{2,1,0:T(8,128)S(1)} %get-tuple-element.130, f32[1,256,256]{2,1,0:T(8,128)S(1)} %get-tuple-element.129), kind=kOutput, calls=%fused_computation.36 | convolution fusion | flops 403832832 | bytes 1900548 | tf_op jit(solution)/shard_map/...ij,...jk->...ik/dot_general | solution.py:12
  14.7 1.2 %maximum_bitcast_fusion.33 = (f32[256,512]{0,1:T(8,128)S(1)}, f32[256,512]{0,1:T(8,128)S(1)}) fusion(f32[1,256,256]{1,2,0:T(8,128)S(1)} %get-tuple-element.191, f32[1,256,256]{1,2,0:T(8,128)} %get-tuple-element.193, f32[1,256,256]{1,2,0:T(8,128)S(1)} %get-tuple-element.192), kind=kLoop, calls=%fused_computation.194 | loop fusion | flops 262144 | bytes 1835008 | tf_op jit(solution)/shard_map/concatenate | solution.py:22
  15.9 1.0 %convolution_bitcast_fusion.10 = f32[1,512,256]{2,1,0:T(8,128)S(1)} fusion(f32[512,256]{0,1:T(8,128)S(1)} %copy-done.1, f32[256,512]{0,1:T(8,128)S(1)} %get-tuple-element.229, f32[256,512]{0,1:T(8,128)S(1)} %get-tuple-element.228, f32[]{:T(128)} %bitcast.21), kind=kOutput, calls=%fused_computation.62 | convolution fusion | flops 403177472 | bytes 2097156 | tf_op jit(solution)/shard_map/...ij,...jk->...ik/dot_general | solution.py:12
  16.9 3.3 %while.24 = (f32[1,512,256]{2,1,0:T(8,128)S(1)}, f32[]{:T(128)}, s32[]{:T(128)}, f32[1,512,512]{2,1,0:T(8,128)S(1)}, f32[512,256]{1,0:T(8,128)S(1)}, /*index=5*/s32[]{:T(128)}) while((f32[1,512,256]{2,1,0:T(8,128)S(1)}, f32[]{:T(128)}, s32[]{:T(128)}, f32[1,512,512]{2,1,0:T(8,128)S(1)}, f32[512,256]{1,0:T(8,128)S(1)}, ...), condition=%wide.region_4.5_spmd, body=%wide.region_2.4_spmd.sunk | while | flops 1209335808 | bytes 6291549 | solution.py:72
  16.9 1.6 %multiply_reduce_fusion.4 = (f32[]{:T(128)}, f32[512,256]{1,0:T(8,128)S(1)}) fusion(f32[512,256]{1,0:T(8,128)S(1)} %get-tuple-element.340, f32[1,512,256]{2,1,0:T(8,128)S(1)} %get-tuple-element.330, f32[1,512,512]{2,1,0:T(8,128)S(1)} %get-tuple-element.339), kind=kOutput, calls=%fused_computation.12.clone.1 | convolution fusion | flops 805699584 | bytes 2621444 | tf_op jit(solution)/shard_map/while/body/...ij,...jk->...ik/dot_general | solution.py:12
  18.5 0.7 fusion.218
  20.6 1.0 %convolution_bitcast_fusion.9 = f32[1,512,256]{1,2,0:T(8,128)S(1)} fusion(f32[256,256]{1,0:T(8,128)S(1)} %get-tuple-element.212, f32[256,256]{1,0:T(8,128)S(1)} %get-tuple-element.128, f32[256,256]{1,0:T(8,128)S(1)} %neg.110, f32[1,512,256]{2,1,0:T(8,128)S(1)} %get-tuple-element.59), kind=kOutput, calls=%fused_computation.61 | convolution fusion | flops 403439616 | bytes 1835008 | tf_op jit(solution)/shard_map/...ij,...jk->...ik/dot_general | solution.py:12
  21.8 1.0 %convolution_bitcast_fusion.8 = f32[1,512,256]{2,1,0:T(8,128)S(1)} fusion(f32[1,256,256]{1,2,0:T(8,128)S(1)} %get-tuple-element.190, f32[1,256,256]{1,2,0:T(8,128)S(1)} %get-tuple-element.189, f32[1,256,256]{1,2,0:T(8,128)S(1)} %get-tuple-element.188, f32[256,256]{0,1:T(8,128)S(1)} %get-tuple-element.127, f32[256,256]{0,1:T(8,128)S(1)} %bitcast.388), kind=kOutput, calls=%fused_computation.60 | convolution fusion | flops 403570688 | bytes 1835008 | tf_op jit(solution)/shard_map/...ij,...jk->...ik/dot_general | solution.py:12
  23.6 1.0 %convolution_bitcast_fusion.5 = f32[1,512,256]{1,2,0:T(8,128)S(1)} fusion(f32[512,256]{1,0:T(8,128)S(1)} %fusion.86, f32[256,256]{1,0:T(8,128)S(1)} %get-tuple-element.212, f32[256,256]{1,0:T(8,128)S(1)} %get-tuple-element.128, f32[256,256]{1,0:T(8,128)S(1)} %neg.110), kind=kOutput, calls=%fused_computation.57 | convolution fusion | flops 403439616 | bytes 1835008 | tf_op jit(solution)/shard_map/...ij,...jk->...ik/dot_general | solution.py:12
  24.7 1.8 %convolution_bitcast_fusion.4 = f32[1,512,256]{2,1,0:T(8,128)} fusion(f32[1,256,256]{1,2,0:T(8,128)S(1)} %get-tuple-element.155, f32[1,256,256]{1,2,0:T(8,128)S(1)} %get-tuple-element.154, f32[1,256,256]{1,2,0:T(8,128)S(1)} %get-tuple-element.153, f32[256,256]{0,1:T(8,128)S(1)} %get-tuple-element.127, f32[256,256]{0,1:T(8,128)S(1)} %bitcast.389), kind=kOutput, calls=%fused_computation.56 | convolution fusion | flops 403570688 | bytes 1835008 | tf_op jit(solution)/shard_map/...ij,...jk->...ik/dot_general | solution.py:12
  29.8 0.7 reduce_max.21
  35.8 0.8 %fusion.72 = f32[512,256]{0,1:T(8,128)S(1)} fusion(f32[512,256]{0,1:T(8,128)S(1)} %select_subtract_fusion.2, f32[256,512]{0,1:T(8,128)S(1)} %get-tuple-element.221, f32[256,512]{0,1:T(8,128)S(1)} %get-tuple-element.220, f32[]{:T(128)} %bitcast.66), kind=kOutput, calls=%fused_computation.133 | convolution fusion | flops 403177472 | bytes 2097156 | tf_op jit(solution)/shard_map/...ij,...jk->...ik/dot_general | solution.py:12
  39.0 1.0 %convolution_bitcast_fusion.6 = f32[1,512,256]{2,1,0:T(8,128)S(1)} fusion(f32[512,256]{0,1:T(8,128)S(1)} %select_subtract_fusion, f32[256,512]{0,1:T(8,128)S(1)} %get-tuple-element.217, f32[256,512]{0,1:T(8,128)S(1)} %get-tuple-element.216, f32[]{:T(128)} %bitcast.64), kind=kOutput, calls=%fused_computation.58 | convolution fusion | flops 403177472 | bytes 2097156 | tf_op jit(solution)/shard_map/...ij,...jk->...ik/dot_general | solution.py:12
  40.0 3.2 %while.25 = (f32[1,512,256]{2,1,0:T(8,128)S(1)}, f32[]{:T(128)}, s32[]{:T(128)}, f32[1,512,512]{2,1,0:T(8,128)S(1)}, f32[512,256]{1,0:T(8,128)S(1)}, /*index=5*/s32[]{:T(128)}) while((f32[1,512,256]{2,1,0:T(8,128)S(1)}, f32[]{:T(128)}, s32[]{:T(128)}, f32[1,512,512]{2,1,0:T(8,128)S(1)}, f32[512,256]{1,0:T(8,128)S(1)}, ...), condition=%wide.region_9.0_spmd, body=%wide.region_7.0_spmd.sunk | while | flops 1209335808 | bytes 6291549 | solution.py:72
  40.0 1.7 %multiply_reduce_fusion.5 = (f32[]{:T(128)}, f32[512,256]{1,0:T(8,128)S(1)}) fusion(f32[512,256]{1,0:T(8,128)S(1)} %get-tuple-element.358, f32[1,512,256]{2,1,0:T(8,128)S(1)} %get-tuple-element.348, f32[1,512,512]{2,1,0:T(8,128)S(1)} %get-tuple-element.357), kind=kOutput, calls=%fused_computation.27.clone.1 | convolution fusion | flops 805699584 | bytes 2621444 | tf_op jit(solution)/shard_map/while/body/...ij,...jk->...ik/dot_general | solution.py:12
  41.8 0.7 fusion.220
  43.6 1.1 %fusion.178 = (f32[1,256,256]{2,1,0:T(8,128)S(1)}, f32[1,256,256]{2,1,0:T(8,128)S(1)}) fusion(f32[1,512,256]{2,1,0:T(8,128)} %collective-permute-done.1, f32[256]{0:T(256)S(1)} %mul.713), kind=kLoop, calls=%fused_computation.354 | loop fusion | flops 196608 | bytes 1049600 | tf_op jit(solution)/shard_map/slice | solution.py:31
  45.4 1.0 %convolution_bitcast_fusion.2 = f32[1,512,256]{2,1,0:T(8,128)S(1)} fusion(f32[1,256,256]{1,2,0:T(8,128)S(1)} %get-tuple-element.150, f32[1,256,256]{1,2,0:T(8,128)S(1)} %get-tuple-element.149, f32[1,256,256]{1,2,0:T(8,128)S(1)} %get-tuple-element.148, f32[1,256,256]{2,1,0:T(8,128)S(1)} %bitcast_negate_fusion, f32[1,256,256]{2,1,0:T(8,128)S(1)} %bitcast.379), kind=kOutput, calls=%fused_computation.54 | convolution fusion | flops 403570688 | bytes 1835008 | tf_op jit(solution)/shard_map/...ij,...jk->...ik/dot_general | solution.py:12
  46.7 32.4 %all_to_all.5 = f32[16,1,4,16,256]{4,3,2,1,0:T(8,128)S(1)} all-to-all(f32[16,1,4,16,256]{4,3,2,1,0:T(8,128)S(1)} %maximum_bitcast_fusion.22), channel_id=1, replica_groups=mesh['groups'=2,'energy'=8,'space'=2] {'energy','space'}, dimensions={0} | all-to-all | bytes 2097152 | tf_op jit(solution)/shard_map/all_to_all | solution.py:129
  79.8 0.8 %copy.56 = f32[8,2,2,16,256]{4,3,2,1,0:T(8,128)} copy(f32[8,2,2,16,256]{4,3,1,2,0:T(8,128)S(1)} %pad_maximum_fusion.1) | data formatting | bytes 1048576 | tf_op jit(solution)/shard_map/stack | solution.py:146
  (115 shorter events, 21.4 us)
Async XLA Ops:
  0.0 0.7 copy-start.3
  0.1 0.7 copy-start.2
  14.7 1.2 %copy-start.1 = (f32[512,256]{0,1:T(8,128)S(1)}, f32[512,256]{0,1:T(8,128)}, u32[]{:S(2)}) copy-start(f32[512,256]{0,1:T(8,128)} %select_subtract_fusion.6) | copy-start | bytes 1572868
  16.9 3.3 %copy-start = (f32[1,2,256,256]{3,2,1,0:T(8,128)S(1)}, f32[1,2,256,256]{3,2,1,0:T(8,128)}, u32[]{:S(2)}) copy-start(f32[1,2,256,256]{3,2,1,0:T(8,128)} %param.10) | copy-start | bytes 1572868
  21.8 1.1 %copy-start.4 = (f32[1,1,256]{2,1,0:T(1,128)S(1)}, f32[1,1,256]{2,1,0:T(1,128)}, u32[]{:S(2)}) copy-start(f32[1,1,256]{2,1,0:T(1,128)} %param.13) | copy-start | bytes 3076
  22.8 4.2 %collective-permute-start = (f32[1,512,256]{2,1,0:T(8,128)S(1)}, f32[1,512,256]{2,1,0:T(8,128)S(1)}, u32[]{:S(2)}, u32[]{:S(2)}) collective-permute-start(f32[1,512,256]{2,1,0:T(8,128)S(1)} %convolution_bitcast_fusion.8), channel_id=1, source_target_pairs={{0,1},{1,0},{2,3},{3,2},{4,5},{5,4},{6,7},{7,6},{8,9},{9,8},{10,11... | collective-permute-start | bytes 1572872 | tf_op jit(solution)/shard_map/ppermute | solution.py:8
  26.5 17.1 %collective-permute-start.1 = (f32[1,512,256]{2,1,0:T(8,128)}, f32[1,512,256]{2,1,0:T(8,128)}, u32[]{:S(2)}, u32[]{:S(2)}) collective-permute-start(f32[1,512,256]{2,1,0:T(8,128)} %convolution_bitcast_fusion.4), channel_id=1, source_target_pairs={{0,1},{1,0},{2,3},{3,2},{4,5},{5,4},{6,7},{7,6},{8,9},{9,8},{10,11... | collective-permute-start | bytes 1572872 | tf_op jit(solution)/shard_map/ppermute | solution.py:8
where the time goes:
time: 82.2 us; the launch traced here: 80.6 us
  blocking collectives  32.4 us (39%)
  matrix products  30.9 us (38%)
  other arithmetic  9.38 us (11%)
  between operations  3.41 us (4%)
  local copies, waits for them, and re-layouts  2.38 us (3%)
  loops' own time  1.62 us (2%)
    all_to_all x1, blocking collectives, body(): lax.all_to_all(paired, ('energy', 'space'), split_axis=0, concat_axis=0,...  32.4 us
    dot_general x35, matrix products, dot(): return jnp.einsum('...ij,...jk->...ik', left, right, precision=precision)  28.4 us
    neg x23, other arithmetic, embed(): top = jnp.concatenate([real, -imag], axis=-1)  3.15 us
    concatenate x12, other arithmetic, embed(): return jnp.concatenate([top, bottom], axis=-2)  2.28 us
  transfers between devices with their start and end apart: 2, of which 0 were waited for; matrix products, arithmetic and copies ran while one was open for 22% of the time, Pallas kernels for 0%

commit v1 on v0

--- a/solution.py
+++ b/solution.py
@@ -69,9 +69,8 @@
         residual = jnp.sqrt(jnp.max(jnp.sum(rest * rest, axis=(-1, -2))))
         return approx + dot(embed(*split(approx)), rest, high), residual, count + 1
 
-    approx, _, _ = lax.while_loop(
-        keep_going, newton, (approx, jnp.float32(jnp.inf), jnp.int32(0))
-    )
+    state = newton((approx, None, jnp.int32(0)))
+    approx, _, _ = lax.while_loop(keep_going, newton, state)
     return approx
 
 

time: 82.2 us -> 85 us (1.034); the launches traced: 80.6 us -> 85.2 us
  local copies, waits for them, and re-layouts: 2.38 us -> 5.56 us
  blocking collectives: 32.4 us -> 35.5 us
  other arithmetic: 9.38 us -> 7.55 us
  between operations: 3.41 us -> 4.86 us
  loops' own time: 1.62 us -> 0.2 us
    all_to_all x1, blocking collectives: 32.4 us -> 35.5 us  [body(): lax.all_to_all(paired, ('energy', 'space'), split_axis=0, concat_axis=0,...]
    while x1 -> x3, local copies, waits for them, and re-layouts: 0.19 us -> 1.63 us  [invert(): approx, _, _ = lax.while_loop(keep_going, newton, state)]
    another operation x2, loops' own time: 1.62 us -> 0.2 us  [invert(): approx, _, _ = lax.while_loop(keep_going, newton, state)]
    concatenate x12, other arithmetic: 2.28 us -> 1.2 us  [embed(): return jnp.concatenate([top, bottom], axis=-2)]
    squeeze x2, local copies, waits for them, and re-layouts: 0.16 us -> 1.2 us  [body(): link_im = jnp.where(first, -swap(link[1]), link[1])]
  transfers between devices with their start and end apart: 2 -> 2, of which waited for: 0 -> 0; matrix products, arithmetic and copies ran while one was open for 22% -> 21% of each run, Pallas kernels for 0% -> 0%
where the time goes in v1:
time: 85 us; the launch traced here: 85.2 us
  blocking collectives  35.5 us (42%)
  matrix products  31 us (36%)
  other arithmetic  7.55 us (9%)
  local copies, waits for them, and re-layouts  5.56 us (7%)
  between operations  4.86 us (6%)
    all_to_all x1, blocking collectives, body(): lax.all_to_all(paired, ('energy', 'space'), split_axis=0, concat_axis=0,...  35.5 us
    dot_general x35, matrix products, dot(): return jnp.einsum('...ij,...jk->...ik', left, right, precision=precision)  28.5 us
    neg x23, other arithmetic, embed(): top = jnp.concatenate([real, -imag], axis=-1)  2.45 us
  transfers between devices with their start and end apart: 2, of which 0 were waited for; matrix products, arithmetic and copies ran while one was open for 21% of the time, Pallas kernels for 0%

profile of v1, /device:TPU:1, one launch (start us, length us, event | category | flops | bytes accessed | tf_op | source)
XLA Modules:
  0.0 85.2 jit_solution(6365075538897626301)
XLA Ops:
  0.1 0.7 copy-done.2
  0.7 1.2 %fusion.196 = (f32[1,256,256]{2,1,0:T(8,128)S(1)}, f32[1,256,256]{2,1,0:T(8,128)S(1)}, f32[1,256,256]{2,1,0:T(8,128)S(1)}) fusion(f32[1,2,256,256]{3,2,1,0:T(8,128)} %param.9, f32[256]{0:T(256)S(1)} %bitcast.409, f32[256]{0:T(256)S(1)} %bitcast.413, f32[]{:T(128)S(6)} %add.163), kind=kLoop, calls=%fused_computation.380 | loop fusion | flops 524288 | bytes 1312772 | tf_op jit(solution)/shard_map/neg | solution.py:20
  5.8 0.6 convolution_multiply_fusion.11
  8.7 0.6 fusion.38
  10.1 0.6 fusion.41
  13.7 1.8 %multiply_reduce_fusion.3 = (f32[]{:T(128)}, f32[512,256]{0,1:T(8,128)S(1)}) fusion(f32[512,256]{0,1:T(8,128)S(1)} %fusion.47, f32[1,256,256]{2,1,0:T(8,128)S(1)} %get-tuple-element.221, f32[1,256,256]{2,1,0:T(8,128)S(1)} %get-tuple-element.130, f32[1,256,256]{2,1,0:T(8,128)S(1)} %get-tuple-element.129, pred[256,256]{0,1:T(32,128)(4,1)S(1)} %iota_compare_fusion), kind=kOutput, calls=%fused_computation.248 | convolution fusion | flops 806617088 | bytes 1900548 | tf_op jit(solution)/shard_map/...ij,...jk->...ik/dot_general | solution.py:12
  15.6 1.4 %fusion.21 = f32[1,512,256]{1,2,0:T(8,128)} fusion(f32[512,256]{0,1:T(8,128)S(1)} %fusion.47, f32[512,256]{0,1:T(8,128)S(1)} %get-tuple-element.249, f32[1,256,256]{1,2,0:T(8,128)S(1)} %get-tuple-element.196, f32[1,256,256]{1,2,0:T(8,128)S(1)} %get-tuple-element.195, f32[1,256,256]{1,2,0:T(8,128)S(1)} %get-tuple-element.194), kind=kOutput, calls=%fused_computation.52 | convolution fusion | flops 403570688 | bytes 2359296 | tf_op jit(solution)/shard_map/...ij,...jk->...ik/dot_general | solution.py:12
  17.0 1.2 %copy.49 = f32[1,512,256]{2,1,0:T(8,128)S(1)} copy(f32[1,512,256]{1,2,0:T(8,128)} %fusion.21) | data formatting | bytes 1048576 | tf_op jit(solution)/shard_map/while | solution.py:73
  19.4 1.1 %slice_bitcast_fusion.2 = (f32[256,256]{1,0:T(8,128)S(1)}, f32[256,256]{0,1:T(8,128)S(1)}) fusion(f32[1,2,256,256]{3,2,1,0:T(8,128)} %param.10), kind=kLoop, calls=%fused_computation.276 | loop fusion | bytes 1048576 | tf_op jit(solution)/shard_map/squeeze | solution.py:104
  20.7 0.8 copy-done
  21.6 1.0 %convolution_bitcast_fusion.8 = f32[1,512,256]{1,2,0:T(8,128)S(1)} fusion(f32[256,256]{1,0:T(8,128)S(1)} %get-tuple-element.218, f32[256,256]{1,0:T(8,128)S(1)} %get-tuple-element.128, f32[256,256]{1,0:T(8,128)S(1)} %neg.117, f32[1,512,256]{2,1,0:T(8,128)S(1)} %get-tuple-element.59), kind=kOutput, calls=%fused_computation.66 | convolution fusion | flops 403439616 | bytes 1835008 | tf_op jit(solution)/shard_map/...ij,...jk->...ik/dot_general | solution.py:12
  22.7 1.8 %convolution_bitcast_fusion.7 = f32[1,512,256]{2,1,0:T(8,128)} fusion(f32[1,256,256]{1,2,0:T(8,128)S(1)} %get-tuple-element.193, f32[1,256,256]{1,2,0:T(8,128)S(1)} %get-tuple-element.192, f32[1,256,256]{1,2,0:T(8,128)S(1)} %get-tuple-element.191, f32[256,256]{0,1:T(8,128)S(1)} %get-tuple-element.127, f32[256,256]{0,1:T(8,128)S(1)} %bitcast.407), kind=kOutput, calls=%fused_computation.65 | convolution fusion | flops 403570688 | bytes 1835008 | tf_op jit(solution)/shard_map/...ij,...jk->...ik/dot_general | solution.py:12
  25.3 1.0 %convolution_bitcast_fusion.5 = f32[1,512,256]{1,2,0:T(8,128)S(1)} fusion(f32[512,256]{1,0:T(8,128)S(1)} %fusion.102, f32[256,256]{1,0:T(8,128)S(1)} %get-tuple-element.218, f32[256,256]{1,0:T(8,128)S(1)} %get-tuple-element.128, f32[256,256]{1,0:T(8,128)S(1)} %neg.117), kind=kOutput, calls=%fused_computation.63 | convolution fusion | flops 403439616 | bytes 1835008 | tf_op jit(solution)/shard_map/...ij,...jk->...ik/dot_general | solution.py:12
  26.4 1.8 %convolution_bitcast_fusion.4 = f32[1,512,256]{2,1,0:T(8,128)} fusion(f32[1,256,256]{1,2,0:T(8,128)S(1)} %get-tuple-element.155, f32[1,256,256]{1,2,0:T(8,128)S(1)} %get-tuple-element.154, f32[1,256,256]{1,2,0:T(8,128)S(1)} %get-tuple-element.153, f32[256,256]{0,1:T(8,128)S(1)} %get-tuple-element.127, f32[256,256]{0,1:T(8,128)S(1)} %bitcast.408), kind=kOutput, calls=%fused_computation.62 | convolution fusion | flops 403570688 | bytes 1835008 | tf_op jit(solution)/shard_map/...ij,...jk->...ik/dot_general | solution.py:12
  33.2 0.6 convolution_multiply_fusion.5
  36.0 0.6 fusion.78
  37.5 0.8 fusion.81
  39.1 0.6 fusion.84
  40.6 0.6 fusion.87
  41.3 1.7 %multiply_reduce_fusion.2 = (f32[]{:T(128)}, f32[512,256]{0,1:T(8,128)S(1)}) fusion(f32[512,512]{1,0:T(8,128)S(1)} %maximum_subtract_fusion, f32[512,256]{0,1:T(8,128)S(1)} %fusion.87, pred[256,256]{0,1:T(32,128)(4,1)S(1)} %iota_compare_fusion), kind=kOutput, calls=%fused_computation.241 | convolution fusion | flops 805830656 | bytes 2162692 | tf_op jit(solution)/shard_map/...ij,...jk->...ik/dot_general | solution.py:12
  45.0 1.1 %fusion.197 = (f32[1,256,256]{2,1,0:T(8,128)S(1)}, f32[1,256,256]{2,1,0:T(8,128)S(1)}) fusion(f32[1,512,256]{2,1,0:T(8,128)} %collective-permute-done.1, f32[256]{0:T(256)S(1)} %mul.723), kind=kLoop, calls=%fused_computation.381 | loop fusion | flops 196608 | bytes 1049600 | tf_op jit(solution)/shard_map/slice | solution.py:31
  46.8 1.0 %convolution_bitcast_fusion.2 = f32[1,512,256]{2,1,0:T(8,128)S(1)} fusion(f32[1,256,256]{1,2,0:T(8,128)S(1)} %get-tuple-element.150, f32[1,256,256]{1,2,0:T(8,128)S(1)} %get-tuple-element.149, f32[1,256,256]{1,2,0:T(8,128)S(1)} %get-tuple-element.148, f32[1,256,256]{2,1,0:T(8,128)S(1)} %bitcast_negate_fusion, f32[1,256,256]{2,1,0:T(8,128)S(1)} %bitcast.398), kind=kOutput, calls=%fused_computation.60 | convolution fusion | flops 403570688 | bytes 1835008 | tf_op jit(solution)/shard_map/...ij,...jk->...ik/dot_general | solution.py:12
  48.0 35.5 %all_to_all.5 = f32[16,1,4,16,256]{4,3,2,1,0:T(8,128)S(1)} all-to-all(f32[16,1,4,16,256]{4,3,2,1,0:T(8,128)S(1)} %maximum_bitcast_fusion.26), channel_id=1, replica_groups=mesh['groups'=2,'energy'=8,'space'=2] {'energy','space'}, dimensions={0} | all-to-all | bytes 2097152 | tf_op jit(solution)/shard_map/all_to_all | solution.py:128
  84.3 0.8 copy.74
  (115 shorter events, 21.1 us)
Async XLA Ops:
  0.0 0.7 copy-start.2
  0.1 0.7 copy-start.1
  20.4 1.0 %copy-start = (f32[1,2,256,256]{3,2,1,0:T(8,128)S(1)}, f32[1,2,256,256]{3,2,1,0:T(8,128)}, u32[]{:S(2)}) copy-start(f32[1,2,256,256]{3,2,1,0:T(8,128)} %param.10) | copy-start | bytes 1572868
  22.7 1.8 %copy-start.3 = (f32[1,1,256]{2,1,0:T(1,128)S(1)}, f32[1,1,256]{2,1,0:T(1,128)}, u32[]{:S(2)}) copy-start(f32[1,1,256]{2,1,0:T(1,128)} %param.13) | copy-start | bytes 3076
  24.5 4.2 %collective-permute-start = (f32[1,512,256]{2,1,0:T(8,128)}, f32[1,512,256]{2,1,0:T(8,128)S(1)}, u32[]{:S(2)}, u32[]{:S(2)}) collective-permute-start(f32[1,512,256]{2,1,0:T(8,128)} %convolution_bitcast_fusion.7), channel_id=1, source_target_pairs={{0,1},{1,0},{2,3},{3,2},{4,5},{5,4},{6,7},{7,6},{8,9},{9,8},{10,11... | collective-permute-start | bytes 1572872 | tf_op jit(solution)/shard_map/ppermute | solution.py:8
  28.2 16.8 %collective-permute-start.1 = (f32[1,512,256]{2,1,0:T(8,128)}, f32[1,512,256]{2,1,0:T(8,128)}, u32[]{:S(2)}, u32[]{:S(2)}) collective-permute-start(f32[1,512,256]{2,1,0:T(8,128)} %convolution_bitcast_fusion.4), channel_id=1, source_target_pairs={{0,1},{1,0},{2,3},{3,2},{4,5},{5,4},{6,7},{7,6},{8,9},{9,8},{10,11... | collective-permute-start | bytes 1572872 | tf_op jit(solution)/shard_map/ppermute | solution.py:8

commit v2 on v0

--- a/solution.py
+++ b/solution.py
@@ -134,15 +134,13 @@
     regrouped = arrived.reshape((total, lax.axis_size("space"), 2, 2, row_count, order))
     a_re, a_im = regrouped[:, :, 0, 0], regrouped[:, :, 0, 1]
     b_re, b_im = regrouped[:, :, 1, 0], regrouped[:, :, 1, 1]
-    corr_re = []
-    corr_im = []
-    for shift_index in range(total):
-        upper_re, upper_im = a_re[shift_index:], a_im[shift_index:]
-        lower_re, lower_im = b_re[: total - shift_index], b_im[: total - shift_index]
-        corr_re.append(jnp.sum(upper_re * lower_re + upper_im * lower_im, axis=0))
-        corr_im.append(jnp.sum(upper_im * lower_re - upper_re * lower_im, axis=0))
-    corr_re = jnp.stack(corr_re, axis=0)
-    corr_im = jnp.stack(corr_im, axis=0)
+    pad = jnp.zeros((total - 1,) + b_re.shape[1:], jnp.float32)
+    padded_re = jnp.concatenate([pad, b_re], axis=0)
+    padded_im = jnp.concatenate([pad, b_im], axis=0)
+    lower_re = jnp.stack([padded_re[total - 1 - k : 2 * total - 1 - k] for k in range(total)])
+    lower_im = jnp.stack([padded_im[total - 1 - k : 2 * total - 1 - k] for k in range(total)])
+    corr_re = jnp.sum(a_re[None] * lower_re + a_im[None] * lower_im, axis=1)
+    corr_im = jnp.sum(a_im[None] * lower_re - a_re[None] * lower_im, axis=1)
     return jnp.stack([-order * corr_im, order * corr_re], axis=2)
 
 

time: 82.2 us -> 83.7 us (1.018); the launches traced: 80.6 us -> 83.3 us
  local copies, waits for them, and re-layouts: 2.38 us -> 3.82 us
    concatenate x12, other arithmetic: 2.28 us -> 1.2 us  [embed(): return jnp.concatenate([top, bottom], axis=-2)]
    transpose x1, local copies, waits for them, and re-layouts: 0.13 us -> 1.08 us  [swap(): return jnp.swapaxes(value, -1, -2)]
where the time goes in v2:
time: 83.7 us; the launch traced here: 83.3 us
  blocking collectives  32.4 us (39%)
  matrix products  31.4 us (38%)
  other arithmetic  10.1 us (12%)
  local copies, waits for them, and re-layouts  3.82 us (5%)
  between operations  3.35 us (4%)
  loops' own time  1.62 us (2%)
    all_to_all x1, blocking collectives, body(): lax.all_to_all(paired, ('energy', 'space'), split_axis=0, concat_axis=0,...  32.4 us
    dot_general x35, matrix products, dot(): return jnp.einsum('...ij,...jk->...ik', left, right, precision=precision)  28.9 us
    neg x23, other arithmetic, embed(): top = jnp.concatenate([real, -imag], axis=-1)  3.18 us
  transfers between devices with their start and end apart: 2, of which 0 were waited for; matrix products, arithmetic and copies ran while one was open for 22% of the time, Pallas kernels for 0%

profile of v2, /device:TPU:1, one launch (start us, length us, event | category | flops | bytes accessed | tf_op | source)
XLA Modules:
  0.0 83.3 jit_solution(17003610536562736211)
XLA Ops:
  0.0 1.2 %fusion.203 = (f32[1,256,256]{2,1,0:T(8,128)S(1)}, f32[1,256,256]{2,1,0:T(8,128)S(1)}, f32[1,256,256]{2,1,0:T(8,128)S(1)}) fusion(f32[1,2,256,256]{3,2,1,0:T(8,128)} %param.9, f32[256]{0:T(256)} %bitcast.395, f32[256]{0:T(256)} %bitcast.399, f32[]{:T(128)S(6)} %add.111), kind=kLoop, calls=%fused_computation.366 | loop fusion | flops 524288 | bytes 1312772 | tf_op jit(solution)/shard_map/neg | solution.py:20
  5.4 0.7 slice_bitcast_fusion.4
  6.2 1.1 %copy.13 = f32[256,256]{1,0:T(8,128)S(1)} copy(f32[256,256]{0,1:T(8,128)} %get-tuple-element.196) | data formatting | bytes 524288 | tf_op jit(solution)/shard_map/transpose | solution.py:16
  7.3 0.9 %negate_bitcast_fusion = (f32[256,256]{0,1:T(8,128)}, f32[256,256]{1,0:T(8,128)S(1)}, f32[256,256]{1,0:T(8,128)}) fusion(f32[1,2,256,256]{3,2,1,0:T(8,128)S(1)} %copy-done, f32[256,256]{0,1:T(8,128)S(1)} %copy.14, pred[]{:T(512)S(6)} %eq.37, f32[256,256]{1,0:T(8,128)S(1)} %copy.13), kind=kLoop, calls=%fused_computation.363 | loop fusion | flops 262144 | bytes 1835009 | tf_op jit(solution)/shard_map/neg | solution.py:35
  8.2 0.7 copy-done.1
  8.9 0.7 neg.110
  16.9 1.0 %convolution_bitcast_fusion.10 = f32[1,512,256]{2,1,0:T(8,128)S(1)} fusion(f32[512,256]{0,1:T(8,128)S(1)} %select_subtract_fusion.6, f32[256,512]{0,1:T(8,128)S(1)} %get-tuple-element.211, f32[256,512]{0,1:T(8,128)S(1)} %get-tuple-element.210, f32[]{:T(128)} %bitcast.21), kind=kOutput, calls=%fused_computation.64 | convolution fusion | flops 403177472 | bytes 2097156 | tf_op jit(solution)/shard_map/...ij,...jk->...ik/dot_general | solution.py:12
  17.9 3.3 %while.24 = (f32[1,512,256]{2,1,0:T(8,128)S(1)}, f32[]{:T(128)}, s32[]{:T(128)}, f32[1,512,512]{2,1,0:T(8,128)S(1)}, f32[512,256]{1,0:T(8,128)S(1)}, /*index=5*/s32[]{:T(128)}) while((f32[1,512,256]{2,1,0:T(8,128)S(1)}, f32[]{:T(128)}, s32[]{:T(128)}, f32[1,512,512]{2,1,0:T(8,128)S(1)}, f32[512,256]{1,0:T(8,128)S(1)}, ...), condition=%wide.region_4.5_spmd, body=%wide.region_2.4_spmd.sunk | while | flops 1209335808 | bytes 6291549 | solution.py:72
  17.9 1.6 %multiply_reduce_fusion.4 = (f32[]{:T(128)}, f32[512,256]{1,0:T(8,128)S(1)}) fusion(f32[512,256]{1,0:T(8,128)S(1)} %get-tuple-element.322, f32[1,512,256]{2,1,0:T(8,128)S(1)} %get-tuple-element.312, f32[1,512,512]{2,1,0:T(8,128)S(1)} %get-tuple-element.321), kind=kOutput, calls=%fused_computation.12.clone.1 | convolution fusion | flops 805699584 | bytes 2621444 | tf_op jit(solution)/shard_map/while/body/...ij,...jk->...ik/dot_general | solution.py:12
  20.3 0.7 fusion.244
  21.3 2.3 %convolution_bitcast_fusion.9 = f32[1,512,256]{1,2,0:T(8,128)S(1)} fusion(f32[256,256]{1,0:T(8,128)} %get-tuple-element.194, f32[256,256]{1,0:T(8,128)} %copy-done.1, f32[256,256]{1,0:T(8,128)} %neg.110, f32[1,512,256]{2,1,0:T(8,128)S(1)} %get-tuple-element.59), kind=kOutput, calls=%fused_computation.63 | convolution fusion | flops 403439616 | bytes 1835008 | tf_op jit(solution)/shard_map/...ij,...jk->...ik/dot_general | solution.py:12
  23.7 1.0 %convolution_bitcast_fusion.8 = f32[1,512,256]{2,1,0:T(8,128)S(1)} fusion(f32[1,256,256]{1,2,0:T(8,128)S(1)} %get-tuple-element.172, f32[1,256,256]{1,2,0:T(8,128)S(1)} %get-tuple-element.171, f32[1,256,256]{1,2,0:T(8,128)S(1)} %get-tuple-element.170, f32[256,256]{0,1:T(8,128)S(1)} %copy-done.6, f32[256,256]{0,1:T(8,128)S(1)} %bitcast.393), kind=kOutput, calls=%fused_computation.62 | convolution fusion | flops 403570688 | bytes 1835008 | tf_op jit(solution)/shard_map/...ij,...jk->...ik/dot_general | solution.py:12
  25.8 1.0 %convolution_bitcast_fusion.5 = f32[1,512,256]{1,2,0:T(8,128)S(1)} fusion(f32[512,256]{1,0:T(8,128)S(1)} %fusion.86, f32[256,256]{1,0:T(8,128)S(1)} %copy-done.7, f32[256,256]{1,0:T(8,128)S(1)} %copy-done.2, f32[256,256]{1,0:T(8,128)S(1)} %copy-done.5), kind=kOutput, calls=%fused_computation.59 | convolution fusion | flops 403439616 | bytes 1835008 | tf_op jit(solution)/shard_map/...ij,...jk->...ik/dot_general | solution.py:12
  26.9 1.8 %convolution_bitcast_fusion.4 = f32[1,512,256]{2,1,0:T(8,128)} fusion(f32[1,256,256]{1,2,0:T(8,128)S(1)} %get-tuple-element.137, f32[1,256,256]{1,2,0:T(8,128)S(1)} %get-tuple-element.136, f32[1,256,256]{1,2,0:T(8,128)S(1)} %get-tuple-element.135, f32[256,256]{0,1:T(8,128)S(1)} %copy-done.6, f32[256,256]{0,1:T(8,128)S(1)} %bitcast.394), kind=kOutput, calls=%fused_computation.58 | convolution fusion | flops 403570688 | bytes 1835008 | tf_op jit(solution)/shard_map/...ij,...jk->...ik/dot_general | solution.py:12
  32.0 0.7 reduce_max.21
  38.8 0.9 %select_subtract_fusion.1 = f32[512,256]{0,1:T(8,128)S(1)} fusion(f32[512,512]{1,0:T(8,128)S(1)} %maximum_subtract_fusion, f32[512,256]{0,1:T(8,128)S(1)} %fusion.72, pred[256,256]{0,1:T(32,128)(4,1)S(1)} %iota_compare_fusion, f32[]{:T(128)} %bitcast.65), kind=kOutput, calls=%fused_computation.31 | convolution fusion | flops 403046400 | bytes 2162692 | tf_op jit(solution)/shard_map/...ij,...jk->...ik/dot_general | solution.py:12
  41.2 1.0 %convolution_bitcast_fusion.6 = f32[1,512,256]{2,1,0:T(8,128)S(1)} fusion(f32[512,256]{0,1:T(8,128)S(1)} %select_subtract_fusion, f32[256,512]{0,1:T(8,128)S(1)} %get-tuple-element.199, f32[256,512]{0,1:T(8,128)S(1)} %get-tuple-element.198, f32[]{:T(128)} %bitcast.64), kind=kOutput, calls=%fused_computation.60 | convolution fusion | flops 403177472 | bytes 2097156 | tf_op jit(solution)/shard_map/...ij,...jk->...ik/dot_general | solution.py:12
  42.3 3.2 %while.25 = (f32[1,512,256]{2,1,0:T(8,128)S(1)}, f32[]{:T(128)}, s32[]{:T(128)}, f32[1,512,512]{2,1,0:T(8,128)S(1)}, f32[512,256]{1,0:T(8,128)S(1)}, /*index=5*/s32[]{:T(128)}) while((f32[1,512,256]{2,1,0:T(8,128)S(1)}, f32[]{:T(128)}, s32[]{:T(128)}, f32[1,512,512]{2,1,0:T(8,128)S(1)}, f32[512,256]{1,0:T(8,128)S(1)}, ...), condition=%wide.region_9.0_spmd, body=%wide.region_7.0_spmd.sunk | while | flops 1209335808 | bytes 6291549 | solution.py:72
  42.3 1.7 %multiply_reduce_fusion.5 = (f32[]{:T(128)}, f32[512,256]{1,0:T(8,128)S(1)}) fusion(f32[512,256]{1,0:T(8,128)S(1)} %get-tuple-element.340, f32[1,512,256]{2,1,0:T(8,128)S(1)} %get-tuple-element.330, f32[1,512,512]{2,1,0:T(8,128)S(1)} %get-tuple-element.339), kind=kOutput, calls=%fused_computation.27.clone.1 | convolution fusion | flops 805699584 | bytes 2621444 | tf_op jit(solution)/shard_map/while/body/...ij,...jk->...ik/dot_general | solution.py:12
  44.7 0.7 fusion.246
  45.8 1.1 %fusion.204 = (f32[1,256,256]{2,1,0:T(8,128)S(1)}, f32[1,256,256]{2,1,0:T(8,128)S(1)}) fusion(f32[1,512,256]{2,1,0:T(8,128)} %collective-permute-done.1, f32[256]{0:T(256)S(1)} %mul.563), kind=kLoop, calls=%fused_computation.367 | loop fusion | flops 196608 | bytes 1049600 | tf_op jit(solution)/shard_map/slice | solution.py:31
  47.6 1.0 %convolution_bitcast_fusion.2 = f32[1,512,256]{2,1,0:T(8,128)S(1)} fusion(f32[1,256,256]{1,2,0:T(8,128)S(1)} %get-tuple-element.132, f32[1,256,256]{1,2,0:T(8,128)S(1)} %get-tuple-element.131, f32[1,256,256]{1,2,0:T(8,128)S(1)} %get-tuple-element.130, f32[1,256,256]{2,1,0:T(8,128)S(1)} %bitcast_negate_fusion, f32[1,256,256]{2,1,0:T(8,128)S(1)} %bitcast.384), kind=kOutput, calls=%fused_computation.56 | convolution fusion | flops 403570688 | bytes 1835008 | tf_op jit(solution)/shard_map/...ij,...jk->...ik/dot_general | solution.py:12
  48.9 32.4 %all_to_all.5 = f32[16,1,4,16,256]{4,3,2,1,0:T(8,128)S(1)} all-to-all(f32[16,1,4,16,256]{4,3,2,1,0:T(8,128)S(1)} %maximum_bitcast_fusion.22), channel_id=1, replica_groups=mesh['groups'=2,'energy'=8,'space'=2] {'energy','space'}, dimensions={0} | all-to-all | bytes 2097152 | tf_op jit(solution)/shard_map/all_to_all | solution.py:129
  82.4 0.8 pad_maximum_fusion.1
  (119 shorter events, 23.3 us)
Async XLA Ops:
  1.8 0.8 copy-start.3
  3.2 2.1 %copy-start = (f32[1,2,256,256]{3,2,1,0:T(8,128)S(1)}, f32[1,2,256,256]{3,2,1,0:T(8,128)}, u32[]{:S(2)}) copy-start(f32[1,2,256,256]{3,2,1,0:T(8,128)} %param.10) | copy-start | bytes 1572868
  7.3 2.5 %copy-start.4 = (f32[512,256]{0,1:T(8,128)S(1)}, f32[512,256]{0,1:T(8,128)}, u32[]{:S(2)}) copy-start(f32[512,256]{0,1:T(8,128)} %copy-done.3) | copy-start | bytes 1572868
  8.2 0.7 copy-start.1
  21.3 2.4 %copy-start.6 = (f32[256,256]{0,1:T(8,128)S(1)}, f32[256,256]{0,1:T(8,128)}, u32[]{:S(2)}) copy-start(f32[256,256]{0,1:T(8,128)} %get-tuple-element.105) | copy-start | bytes 786436
  21.3 2.4 %copy-start.7 = (f32[256,256]{1,0:T(8,128)S(1)}, f32[256,256]{1,0:T(8,128)}, u32[]{:S(2)}) copy-start(f32[256,256]{1,0:T(8,128)} %get-tuple-element.194) | copy-start | bytes 786436
  23.6 1.2 %copy-start.8 = (f32[1,1,256]{2,1,0:T(1,128)S(1)}, f32[1,1,256]{2,1,0:T(1,128)}, u32[]{:S(2)}) copy-start(f32[1,1,256]{2,1,0:T(1,128)} %param.12) | copy-start | bytes 3076
  23.6 1.2 %copy-start.9 = (f32[1,1,256]{2,1,0:T(1,128)S(1)}, f32[1,1,256]{2,1,0:T(1,128)}, u32[]{:S(2)}) copy-start(f32[1,1,256]{2,1,0:T(1,128)} %param.13) | copy-start | bytes 3076
  24.7 4.5 %collective-permute-start = (f32[1,512,256]{2,1,0:T(8,128)S(1)}, f32[1,512,256]{2,1,0:T(8,128)S(1)}, u32[]{:S(2)}, u32[]{:S(2)}) collective-permute-start(f32[1,512,256]{2,1,0:T(8,128)S(1)} %convolution_bitcast_fusion.8), channel_id=1, source_target_pairs={{0,1},{1,0},{2,3},{3,2},{4,5},{5,4},{6,7},{7,6},{8,9},{9,8},{10,11... | collective-permute-start | bytes 1572872 | tf_op jit(solution)/shard_map/ppermute | solution.py:8
  24.8 1.0 %copy-start.2 = (f32[256,256]{1,0:T(8,128)S(1)}, f32[256,256]{1,0:T(8,128)}, u32[]{:S(2)}) copy-start(f32[256,256]{1,0:T(8,128)} %copy-done.1) | copy-start | bytes 786436
  24.8 1.0 %copy-start.5 = (f32[256,256]{1,0:T(8,128)S(1)}, f32[256,256]{1,0:T(8,128)}, u32[]{:S(2)}) copy-start(f32[256,256]{1,0:T(8,128)} %neg.110) | copy-start | bytes 786436
  28.7 17.1 %collective-permute-start.1 = (f32[1,512,256]{2,1,0:T(8,128)}, f32[1,512,256]{2,1,0:T(8,128)}, u32[]{:S(2)}, u32[]{:S(2)}) collective-permute-start(f32[1,512,256]{2,1,0:T(8,128)} %convolution_bitcast_fusion.4), channel_id=1, source_target_pairs={{0,1},{1,0},{2,3},{3,2},{4,5},{5,4},{6,7},{7,6},{8,9},{9,8},{10,11... | collective-permute-start | bytes 1572872 | tf_op jit(solution)/shard_map/ppermute | solution.py:8

commit v3 on v0

--- a/solution.py
+++ b/solution.py
@@ -101,10 +101,15 @@
     g_re, g_im = split(green_col)
     scaled = embed(-g_im * source[:, None, :], g_re * source[:, None, :])
     link = ham_coupling[0]
-    link_re = jnp.where(first, swap(link[0]), link[0])
-    link_im = jnp.where(first, -swap(link[1]), link[1])
-    link_embed = embed(link_re, link_im)
-    link_adj = stacked_adjoint(link_re, link_im)
+    def forms(real, imag):
+        return embed(real, imag), stacked_adjoint(real, imag)
+
+    link_embed, link_adj = lax.cond(
+        first,
+        lambda pair: forms(swap(pair[0]), -swap(pair[1])),
+        lambda pair: forms(pair[0], pair[1]),
+        link,
+    )
     high = lax.Precision.HIGH
     left_green = dot(link_embed, green_col, high)
     coupled_green = from_partner(dot(embed(*split(left_green)), link_adj, high), "space", 0)

time: 82.2 us -> 83.7 us (1.018); the launches traced: 80.6 us -> 85.1 us
  blocking collectives: 32.4 us -> 34.9 us
  other arithmetic: 9.38 us -> 11.2 us
    all_to_all x1, blocking collectives: 32.4 us -> 34.9 us  [body(): lax.all_to_all(paired, ('energy', 'space'), split_axis=0, concat_axis=0,...]
    concatenate x12 -> x13, other arithmetic: 2.28 us -> 3.36 us  [embed(): return jnp.concatenate([top, bottom], axis=-2)]
    neg x23 -> x22, other arithmetic: 3.15 us -> 3.12 us  [embed(): top = jnp.concatenate([real, -imag], axis=-1)]
  transfers between devices with their start and end apart: 2 -> 2, of which waited for: 0 -> 0; matrix products, arithmetic and copies ran while one was open for 22% -> 21% of each run, Pallas kernels for 0% -> 0%
where the time goes in v3:
time: 83.7 us; the launch traced here: 85.1 us
  blocking collectives  34.9 us (42%)
  matrix products  30.9 us (37%)
  other arithmetic  11.2 us (13%)
  between operations  3.31 us (4%)
  local copies, waits for them, and re-layouts  2.58 us (3%)
  loops' own time  1.61 us (2%)
    all_to_all x1, blocking collectives, body(): lax.all_to_all(paired, ('energy', 'space'), split_axis=0, concat_axis=0,...  34.9 us
    dot_general x35, matrix products, dot(): return jnp.einsum('...ij,...jk->...ik', left, right, precision=precision)  28.4 us
    concatenate x13, other arithmetic, embed(): return jnp.concatenate([top, bottom], axis=-2)  3.36 us
    neg x22, other arithmetic, embed(): top = jnp.concatenate([real, -imag], axis=-1)  3.12 us
  transfers between devices with their start and end apart: 2, of which 0 were waited for; matrix products, arithmetic and copies ran while one was open for 21% of the time, Pallas kernels for 0%

profile of v3, /device:TPU:1, one launch (start us, length us, event | category | flops | bytes accessed | tf_op | source)
XLA Modules:
  0.0 85.1 jit_solution(4654126324116031102)
XLA Ops:
  0.7 1.2 %fusion.177 = (f32[1,256,256]{2,1,0:T(8,128)S(1)}, f32[1,256,256]{2,1,0:T(8,128)S(1)}, f32[1,256,256]{2,1,0:T(8,128)S(1)}) fusion(f32[1,2,256,256]{3,2,1,0:T(8,128)} %param.11, f32[256]{0:T(256)S(1)} %bitcast.403, f32[256]{0:T(256)S(1)} %bitcast.407, f32[]{:T(128)S(6)} %add.151), kind=kLoop, calls=%fused_computation.355 | loop fusion | flops 524288 | bytes 1312772 | tf_op jit(solution)/shard_map/neg | solution.py:20
  12.2 0.8 slice_negate_fusion.14
  13.0 1.4 %select_subtract_fusion.6 = f32[512,256]{0,1:T(8,128)} fusion(f32[512,256]{0,1:T(8,128)S(1)} %fusion.44, pred[256,256]{0,1:T(32,128)(4,1)S(1)} %iota_compare_fusion, f32[]{:T(128)} %bitcast.31, f32[1,256,256]{2,1,0:T(8,128)S(1)} %get-tuple-element.224, f32[1,256,256]{2,1,0:T(8,128)S(1)} %get-tuple-element.134, f32[1,256,256]{2,1,0:T(8,128)S(1)} %get-tuple-element.133), kind=kOutput, calls=%fused_computation.47 | convolution fusion | flops 403832832 | bytes 1900548 | tf_op jit(solution)/shard_map/...ij,...jk->...ik/dot_general | solution.py:12
  14.6 1.2 %maximum_bitcast_fusion.33 = (f32[256,512]{0,1:T(8,128)S(1)}, f32[256,512]{0,1:T(8,128)S(1)}) fusion(f32[1,256,256]{1,2,0:T(8,128)S(1)} %get-tuple-element.203, f32[1,256,256]{1,2,0:T(8,128)} %get-tuple-element.205, f32[1,256,256]{1,2,0:T(8,128)S(1)} %get-tuple-element.204), kind=kLoop, calls=%fused_computation.204 | loop fusion | flops 262144 | bytes 1835008 | tf_op jit(solution)/shard_map/concatenate | solution.py:22
  15.8 1.0 %convolution_bitcast_fusion.10 = f32[1,512,256]{2,1,0:T(8,128)S(1)} fusion(f32[512,256]{0,1:T(8,128)S(1)} %copy-done.1, f32[256,512]{0,1:T(8,128)S(1)} %get-tuple-element.238, f32[256,512]{0,1:T(8,128)S(1)} %get-tuple-element.237, f32[]{:T(128)} %bitcast.31), kind=kOutput, calls=%fused_computation.73 | convolution fusion | flops 403177472 | bytes 2097156 | tf_op jit(solution)/shard_map/...ij,...jk->...ik/dot_general | solution.py:12
  16.9 3.1 %while.24 = (f32[1,512,256]{2,1,0:T(8,128)S(1)}, f32[]{:T(128)}, s32[]{:T(128)}, f32[1,512,512]{2,1,0:T(8,128)S(1)}, f32[512,256]{1,0:T(8,128)S(1)}, /*index=5*/s32[]{:T(128)}) while((f32[1,512,256]{2,1,0:T(8,128)S(1)}, f32[]{:T(128)}, s32[]{:T(128)}, f32[1,512,512]{2,1,0:T(8,128)S(1)}, f32[512,256]{1,0:T(8,128)S(1)}, ...), condition=%wide.region_4.5_spmd, body=%wide.region_2.4_spmd.sunk | while | flops 1209335808 | bytes 6291549 | solution.py:72
  16.9 1.6 %multiply_reduce_fusion.4 = (f32[]{:T(128)}, f32[512,256]{1,0:T(8,128)S(1)}) fusion(f32[512,256]{1,0:T(8,128)S(1)} %get-tuple-element.353, f32[1,512,256]{2,1,0:T(8,128)S(1)} %get-tuple-element.343, f32[1,512,512]{2,1,0:T(8,128)S(1)} %get-tuple-element.352), kind=kOutput, calls=%fused_computation.12.clone.1 | convolution fusion | flops 805699584 | bytes 2621444 | tf_op jit(solution)/shard_map/while/body/...ij,...jk->...ik/dot_general | solution.py:12
  18.5 0.7 fusion.223
  20.2 2.5 %conditional.1 = (f32[512,512]{1,0:T(8,128)S(1)}, f32[512,256]{0,1:T(8,128)S(1)}) conditional(s32[]{:T(128)} %convert_element_type.15, f32[2,256,256]{1,2,0:T(8,128)S(1)} %bitcast.379, f32[2,256,256]{1,2,0:T(8,128)S(1)} %bitcast.380), branch_computations={%region_5.0_spmd, %region_6.0_spmd} | conditional | flops 983040 | bytes 6815788 | solution.py:107
  20.6 0.8 fusion.10
  21.5 1.1 %maximum_maximum_fusion = f32[512,512]{1,0:T(8,128)S(1)} fusion(f32[256,256]{1,0:T(8,128)S(1)} %bitcast.388, f32[256,256]{1,0:T(8,128)S(1)} %bitcast.387, f32[256,256]{1,0:T(8,128)} %get-tuple-element.143), kind=kLoop, calls=%fused_computation.15 | loop fusion | flops 786432 | bytes 1835008 | tf_op jit(solution)/shard_map/cond/branch_0_fun/concatenate | solution.py:22
  22.7 1.0 %convolution_bitcast_fusion.9 = f32[1,512,256]{1,2,0:T(8,128)S(1)} fusion(f32[512,512]{1,0:T(8,128)S(1)} %get-tuple-element.64, f32[1,512,256]{2,1,0:T(8,128)S(1)} %get-tuple-element.63), kind=kOutput, calls=%fused_computation.72 | convolution fusion | flops 402653184 | bytes 2097152 | tf_op jit(solution)/shard_map/...ij,...jk->...ik/dot_general | solution.py:12
  23.9 1.0 %convolution_bitcast_fusion.8 = f32[1,512,256]{2,1,0:T(8,128)S(1)} fusion(f32[512,256]{0,1:T(8,128)S(1)} %get-tuple-element.65, f32[1,256,256]{1,2,0:T(8,128)S(1)} %get-tuple-element.202, f32[1,256,256]{1,2,0:T(8,128)S(1)} %get-tuple-element.201, f32[1,256,256]{1,2,0:T(8,128)S(1)} %get-tuple-element.200), kind=kOutput, calls=%fused_computation.71 | convolution fusion | flops 403439616 | bytes 1835008 | tf_op jit(solution)/shard_map/...ij,...jk->...ik/dot_general | solution.py:12
  25.7 1.0 %convolution_bitcast_fusion.5 = f32[1,512,256]{1,2,0:T(8,128)S(1)} fusion(f32[512,256]{1,0:T(8,128)S(1)} %fusion.88, f32[512,512]{1,0:T(8,128)S(1)} %get-tuple-element.64), kind=kOutput, calls=%fused_computation.68 | convolution fusion | flops 402653184 | bytes 2097152 | tf_op jit(solution)/shard_map/...ij,...jk->...ik/dot_general | solution.py:12
  26.8 1.8 %convolution_bitcast_fusion.4 = f32[1,512,256]{2,1,0:T(8,128)} fusion(f32[512,256]{0,1:T(8,128)S(1)} %get-tuple-element.65, f32[1,256,256]{1,2,0:T(8,128)S(1)} %get-tuple-element.167, f32[1,256,256]{1,2,0:T(8,128)S(1)} %get-tuple-element.166, f32[1,256,256]{1,2,0:T(8,128)S(1)} %get-tuple-element.165), kind=kOutput, calls=%fused_computation.67 | convolution fusion | flops 403439616 | bytes 1835008 | tf_op jit(solution)/shard_map/...ij,...jk->...ik/dot_general | solution.py:12
  38.6 0.9 %select_subtract_fusion.1 = f32[512,256]{0,1:T(8,128)S(1)} fusion(f32[512,512]{1,0:T(8,128)S(1)} %maximum_subtract_fusion, f32[512,256]{0,1:T(8,128)S(1)} %fusion.74, pred[256,256]{0,1:T(32,128)(4,1)S(1)} %iota_compare_fusion, f32[]{:T(128)} %bitcast.70), kind=kOutput, calls=%fused_computation.42 | convolution fusion | flops 403046400 | bytes 2162692 | tf_op jit(solution)/shard_map/...ij,...jk->...ik/dot_general | solution.py:12
  41.0 1.0 %convolution_bitcast_fusion.6 = f32[1,512,256]{2,1,0:T(8,128)S(1)} fusion(f32[512,256]{0,1:T(8,128)S(1)} %select_subtract_fusion, f32[256,512]{0,1:T(8,128)S(1)} %get-tuple-element.226, f32[256,512]{0,1:T(8,128)S(1)} %get-tuple-element.225, f32[]{:T(128)} %bitcast.69), kind=kOutput, calls=%fused_computation.69 | convolution fusion | flops 403177472 | bytes 2097156 | tf_op jit(solution)/shard_map/...ij,...jk->...ik/dot_general | solution.py:12
  42.0 3.0 %while.25 = (f32[1,512,256]{2,1,0:T(8,128)S(1)}, f32[]{:T(128)}, s32[]{:T(128)}, f32[1,512,512]{2,1,0:T(8,128)S(1)}, f32[512,256]{1,0:T(8,128)S(1)}, /*index=5*/s32[]{:T(128)}) while((f32[1,512,256]{2,1,0:T(8,128)S(1)}, f32[]{:T(128)}, s32[]{:T(128)}, f32[1,512,512]{2,1,0:T(8,128)S(1)}, f32[512,256]{1,0:T(8,128)S(1)}, ...), condition=%wide.region_11.12_spmd, body=%wide.region_9.11_spmd.sunk | while | flops 1209335808 | bytes 6291549 | solution.py:72
  42.0 1.6 %multiply_reduce_fusion.5 = (f32[]{:T(128)}, f32[512,256]{1,0:T(8,128)S(1)}) fusion(f32[512,256]{1,0:T(8,128)S(1)} %get-tuple-element.371, f32[1,512,256]{2,1,0:T(8,128)S(1)} %get-tuple-element.361, f32[1,512,512]{2,1,0:T(8,128)S(1)} %get-tuple-element.370), kind=kOutput, calls=%fused_computation.38.clone.1 | convolution fusion | flops 805699584 | bytes 2621444 | tf_op jit(solution)/shard_map/while/body/...ij,...jk->...ik/dot_general | solution.py:12
  43.7 0.7 fusion.225
  45.4 1.1 %fusion.179 = (f32[1,256,256]{2,1,0:T(8,128)S(1)}, f32[1,256,256]{2,1,0:T(8,128)S(1)}) fusion(f32[1,512,256]{2,1,0:T(8,128)} %collective-permute-done.1, f32[256]{0:T(256)S(1)} %mul.713), kind=kLoop, calls=%fused_computation.357 | loop fusion | flops 196608 | bytes 1049600 | tf_op jit(solution)/shard_map/slice | solution.py:31
  47.3 1.0 %convolution_bitcast_fusion.2 = f32[1,512,256]{2,1,0:T(8,128)S(1)} fusion(f32[1,256,256]{1,2,0:T(8,128)S(1)} %get-tuple-element.162, f32[1,256,256]{1,2,0:T(8,128)S(1)} %get-tuple-element.161, f32[1,256,256]{1,2,0:T(8,128)S(1)} %get-tuple-element.160, f32[1,256,256]{2,1,0:T(8,128)S(1)} %bitcast_negate_fusion.1, f32[1,256,256]{2,1,0:T(8,128)S(1)} %bitcast.394), kind=kOutput, calls=%fused_computation.65 | convolution fusion | flops 403570688 | bytes 1835008 | tf_op jit(solution)/shard_map/...ij,...jk->...ik/dot_general | solution.py:12
  48.5 34.9 %all_to_all.5 = f32[16,1,4,16,256]{4,3,2,1,0:T(8,128)S(1)} all-to-all(f32[16,1,4,16,256]{4,3,2,1,0:T(8,128)S(1)} %maximum_bitcast_fusion.22), channel_id=1, replica_groups=mesh['groups'=2,'energy'=8,'space'=2] {'energy','space'}, dimensions={0} | all-to-all | bytes 2097152 | tf_op jit(solution)/shard_map/all_to_all | solution.py:134
  84.2 0.8 copy.56
  (120 shorter events, 23.4 us)
Async XLA Ops:
  0.0 0.7 copy-start.4
  0.1 0.7 copy-start.3
  14.6 1.2 %copy-start.1 = (f32[512,256]{0,1:T(8,128)S(1)}, f32[512,256]{0,1:T(8,128)}, u32[]{:S(2)}) copy-start(f32[512,256]{0,1:T(8,128)} %select_subtract_fusion.6) | copy-start | bytes 1572868
  16.8 3.1 %copy-start.2 = (f32[1,2,256,256]{3,2,1,0:T(8,128)S(1)}, f32[1,2,256,256]{3,2,1,0:T(8,128)}, u32[]{:S(2)}) copy-start(f32[1,2,256,256]{3,2,1,0:T(8,128)} %param.12) | copy-start | bytes 1572868
  21.5 1.1 %copy-start = (f32[256,256]{0,1:T(8,128)S(1)}, f32[256,256]{0,1:T(8,128)}, u32[]{:S(2)}) copy-start(f32[256,256]{0,1:T(8,128)} %get-tuple-element.142) | copy-start | bytes 786436 | tf_op jit(solution)/shard_map/cond
  23.8 1.1 %copy-start.5 = (f32[1,1,256]{2,1,0:T(1,128)S(1)}, f32[1,1,256]{2,1,0:T(1,128)}, u32[]{:S(2)}) copy-start(f32[1,1,256]{2,1,0:T(1,128)} %param.15) | copy-start | bytes 3076
  24.9 4.3 %collective-permute-start = (f32[1,512,256]{2,1,0:T(8,128)S(1)}, f32[1,512,256]{2,1,0:T(8,128)S(1)}, u32[]{:S(2)}, u32[]{:S(2)}) collective-permute-start(f32[1,512,256]{2,1,0:T(8,128)S(1)} %convolution_bitcast_fusion.8), channel_id=1, source_target_pairs={{0,1},{1,0},{2,3},{3,2},{4,5},{5,4},{6,7},{7,6},{8,9},{9,8},{10,11... | collective-permute-start | bytes 1572872 | tf_op jit(solution)/shard_map/ppermute | solution.py:8
  28.6 16.8 %collective-permute-start.1 = (f32[1,512,256]{2,1,0:T(8,128)}, f32[1,512,256]{2,1,0:T(8,128)}, u32[]{:S(2)}, u32[]{:S(2)}) collective-permute-start(f32[1,512,256]{2,1,0:T(8,128)} %convolution_bitcast_fusion.4), channel_id=1, source_target_pairs={{0,1},{1,0},{2,3},{3,2},{4,5},{5,4},{6,7},{7,6},{8,9},{9,8},{10,11... | collective-permute-start | bytes 1572872 | tf_op jit(solution)/shard_map/ppermute | solution.py:8

commit v4 on v0

--- a/solution.py
+++ b/solution.py
@@ -48,8 +48,10 @@
     beta = beta[..., None, None]
     lower = 0.25 / beta
     alpha = 2.0 / (lower + 1.0)
-    first_step = 2.0 * eye - (alpha / beta) * gram
-    approx = jnp.einsum("...ji,...jk->...ik", matrix, first_step, precision=high) * (alpha / beta)
+    base = jnp.einsum("...ji,...jk->...ik", matrix, eye, precision=high)
+    cubic = jnp.einsum("...ji,...jk->...ik", matrix, gram, precision=high)
+    scale = alpha / beta
+    approx = (2.0 * scale) * base - (scale * scale) * cubic
     ratio = (1.0 - lower) / (1.0 + lower)
     lower = 1.0 - ratio * ratio
     for _ in range(5):

time: 82.2 us -> 87.2 us (1.061); the launches traced: 80.6 us -> 86.9 us
  blocking collectives: 32.4 us -> 38.7 us
  other arithmetic: 9.38 us -> 7.61 us
  matrix products: 30.9 us -> 31.9 us
    all_to_all x1, blocking collectives: 32.4 us -> 38.7 us  [body(): lax.all_to_all(paired, ('energy', 'space'), split_axis=0, concat_axis=0,...]
    concatenate x12, other arithmetic: 2.28 us -> 1.2 us  [embed(): return jnp.concatenate([top, bottom], axis=-2)]
    dot_general x2 -> x4, matrix products: 1.27 us -> 2.21 us  [the longest x2 1.22 us: invert(): cubic = jnp.einsum('...ji,...jk->...ik', matrix, gram, precision=high)]
    unnamed x24, local copies, waits for them, and re-layouts: 0.79 us -> 1.72 us
  transfers between devices with their start and end apart: 2 -> 2, of which waited for: 0 -> 0; matrix products, arithmetic and copies ran while one was open for 22% -> 21% of each run, Pallas kernels for 0% -> 0%
where the time goes in v4:
time: 87.2 us; the launch traced here: 86.9 us
  blocking collectives  38.7 us (44%)
  matrix products  31.9 us (37%)
  other arithmetic  7.61 us (9%)
  between operations  3.4 us (4%)
  local copies, waits for them, and re-layouts  3.1 us (4%)
  loops' own time  1.62 us (2%)
    all_to_all x1, blocking collectives, body(): lax.all_to_all(paired, ('energy', 'space'), split_axis=0, concat_axis=0,...  38.7 us
    dot_general x35, matrix products, dot(): return jnp.einsum('...ij,...jk->...ik', left, right, precision=precision)  28.5 us
    neg x23, other arithmetic, embed(): top = jnp.concatenate([real, -imag], axis=-1)  2.46 us
  transfers between devices with their start and end apart: 2, of which 0 were waited for; matrix products, arithmetic and copies ran while one was open for 21% of the time, Pallas kernels for 0%

profile of v4, /device:TPU:1, one launch (start us, length us, event | category | flops | bytes accessed | tf_op | source)
XLA Modules:
  0.0 86.9 jit_solution(8192647192554605244)
XLA Ops:
  0.1 0.7 copy-done.3
  0.7 1.2 %fusion.170 = (f32[1,256,256]{2,1,0:T(8,128)S(1)}, f32[1,256,256]{2,1,0:T(8,128)S(1)}, f32[1,256,256]{2,1,0:T(8,128)S(1)}) fusion(f32[1,2,256,256]{3,2,1,0:T(8,128)} %param.9, f32[256]{0:T(256)S(1)} %bitcast.397, f32[256]{0:T(256)S(1)} %bitcast.401, f32[]{:T(128)S(6)} %add.151), kind=kLoop, calls=%fused_computation.346 | loop fusion | flops 524288 | bytes 1312772 | tf_op jit(solution)/shard_map/neg | solution.py:20
  8.4 0.6 select_subtract_fusion.8
  12.8 1.4 %select_subtract_fusion.5 = f32[512,256]{1,0:T(8,128)} fusion(f32[512,256]{0,1:T(8,128)S(1)} %fusion.44, pred[256,256]{1,0:T(32,128)(4,1)S(1)} %iota_compare_fusion, f32[]{:T(128)} %bitcast.21, f32[1,256,256]{2,1,0:T(8,128)S(1)} %get-tuple-element.185, f32[1,256,256]{2,1,0:T(8,128)S(1)} %get-tuple-element.100, f32[1,256,256]{2,1,0:T(8,128)S(1)} %get-tuple-element.99), kind=kOutput, calls=%fused_computation.35 | convolution fusion | flops 403832832 | bytes 1900548 | tf_op jit(solution)/shard_map/...ij,...jk->...ik/dot_general | solution.py:12
  14.3 1.0 %copy-done.1 = f32[512,256]{1,0:T(8,128)S(1)} copy-done((f32[512,256]{1,0:T(8,128)S(1)}, f32[512,256]{1,0:T(8,128)}, u32[]{:S(2)}) %copy-start.1) | copy-done | bytes 524312
  15.3 1.0 %convolution_bitcast_fusion.10 = f32[1,512,256]{2,1,0:T(8,128)S(1)} fusion(f32[512,256]{1,0:T(8,128)S(1)} %copy-done.1, f32[256,512]{0,1:T(8,128)S(1)} %get-tuple-element.199, f32[256,512]{0,1:T(8,128)S(1)} %get-tuple-element.198, f32[]{:T(128)} %bitcast.21), kind=kOutput, calls=%fused_computation.64 | convolution fusion | flops 403177472 | bytes 2097156 | tf_op jit(solution)/shard_map/...ij,...jk->...ik/dot_general | solution.py:12
  16.3 3.3 %while.24 = (f32[1,512,256]{2,1,0:T(8,128)S(1)}, f32[]{:T(128)}, s32[]{:T(128)}, f32[1,512,512]{2,1,0:T(8,128)S(1)}, f32[512,256]{1,0:T(8,128)S(1)}, /*index=5*/s32[]{:T(128)}) while((f32[1,512,256]{2,1,0:T(8,128)S(1)}, f32[]{:T(128)}, s32[]{:T(128)}, f32[1,512,512]{2,1,0:T(8,128)S(1)}, f32[512,256]{1,0:T(8,128)S(1)}, ...), condition=%wide.region_4.5_spmd, body=%wide.region_2.4_spmd.sunk | while | flops 1209335808 | bytes 6291549 | solution.py:74
  16.3 1.6 %multiply_reduce_fusion.4 = (f32[]{:T(128)}, f32[512,256]{1,0:T(8,128)S(1)}) fusion(f32[512,256]{1,0:T(8,128)S(1)} %get-tuple-element.310, f32[1,512,256]{2,1,0:T(8,128)S(1)} %get-tuple-element.300, f32[1,512,512]{2,1,0:T(8,128)S(1)} %get-tuple-element.309), kind=kOutput, calls=%fused_computation.12.clone.1 | convolution fusion | flops 805699584 | bytes 2621444 | tf_op jit(solution)/shard_map/while/body/...ij,...jk->...ik/dot_general | solution.py:12
  18.0 0.7 fusion.214
  20.1 1.0 %convolution_bitcast_fusion.9 = f32[1,512,256]{1,2,0:T(8,128)S(1)} fusion(f32[256,256]{1,0:T(8,128)S(1)} %get-tuple-element.182, f32[256,256]{1,0:T(8,128)S(1)} %get-tuple-element.98, f32[256,256]{1,0:T(8,128)S(1)} %neg.110, f32[1,512,256]{2,1,0:T(8,128)S(1)} %get-tuple-element.59), kind=kOutput, calls=%fused_computation.63 | convolution fusion | flops 403439616 | bytes 1835008 | tf_op jit(solution)/shard_map/...ij,...jk->...ik/dot_general | solution.py:12
  21.2 1.0 %convolution_bitcast_fusion.8 = f32[1,512,256]{2,1,0:T(8,128)S(1)} fusion(f32[1,256,256]{1,2,0:T(8,128)S(1)} %get-tuple-element.160, f32[1,256,256]{1,2,0:T(8,128)S(1)} %get-tuple-element.159, f32[1,256,256]{1,2,0:T(8,128)S(1)} %get-tuple-element.158, f32[256,256]{0,1:T(8,128)S(1)} %get-tuple-element.97, f32[256,256]{0,1:T(8,128)S(1)} %bitcast.395), kind=kOutput, calls=%fused_computation.62 | convolution fusion | flops 403570688 | bytes 1835008 | tf_op jit(solution)/shard_map/...ij,...jk->...ik/dot_general | solution.py:12
  23.0 1.0 %convolution_bitcast_fusion.5 = f32[1,512,256]{1,2,0:T(8,128)S(1)} fusion(f32[512,256]{1,0:T(8,128)S(1)} %fusion.88, f32[256,256]{1,0:T(8,128)S(1)} %get-tuple-element.182, f32[256,256]{1,0:T(8,128)S(1)} %get-tuple-element.98, f32[256,256]{1,0:T(8,128)S(1)} %neg.110), kind=kOutput, calls=%fused_computation.59 | convolution fusion | flops 403439616 | bytes 1835008 | tf_op jit(solution)/shard_map/...ij,...jk->...ik/dot_general | solution.py:12
  24.2 1.8 %convolution_bitcast_fusion.4 = f32[1,512,256]{2,1,0:T(8,128)} fusion(f32[1,256,256]{1,2,0:T(8,128)S(1)} %get-tuple-element.125, f32[1,256,256]{1,2,0:T(8,128)S(1)} %get-tuple-element.124, f32[1,256,256]{1,2,0:T(8,128)S(1)} %get-tuple-element.123, f32[256,256]{0,1:T(8,128)S(1)} %get-tuple-element.97, f32[256,256]{0,1:T(8,128)S(1)} %bitcast.396), kind=kOutput, calls=%fused_computation.58 | convolution fusion | flops 403570688 | bytes 1835008 | tf_op jit(solution)/shard_map/...ij,...jk->...ik/dot_general | solution.py:12
  29.2 0.7 reduce_max.21
  33.6 0.6 select_subtract_fusion.3
  35.8 0.8 fusion.74
  39.0 1.0 %convolution_bitcast_fusion.6 = f32[1,512,256]{2,1,0:T(8,128)S(1)} fusion(f32[512,256]{1,0:T(8,128)S(1)} %select_subtract_fusion, f32[256,512]{0,1:T(8,128)S(1)} %get-tuple-element.187, f32[256,512]{0,1:T(8,128)S(1)} %get-tuple-element.186, f32[]{:T(128)} %bitcast.65), kind=kOutput, calls=%fused_computation.60 | convolution fusion | flops 403177472 | bytes 2097156 | tf_op jit(solution)/shard_map/...ij,...jk->...ik/dot_general | solution.py:12
  40.0 3.2 %while.25 = (f32[1,512,256]{2,1,0:T(8,128)S(1)}, f32[]{:T(128)}, s32[]{:T(128)}, f32[1,512,512]{2,1,0:T(8,128)S(1)}, f32[512,256]{1,0:T(8,128)S(1)}, /*index=5*/s32[]{:T(128)}) while((f32[1,512,256]{2,1,0:T(8,128)S(1)}, f32[]{:T(128)}, s32[]{:T(128)}, f32[1,512,512]{2,1,0:T(8,128)S(1)}, f32[512,256]{1,0:T(8,128)S(1)}, ...), condition=%wide.region_9.0_spmd, body=%wide.region_7.0_spmd.sunk | while | flops 1209335808 | bytes 6291549 | solution.py:74
  40.0 1.7 %multiply_reduce_fusion.5 = (f32[]{:T(128)}, f32[512,256]{1,0:T(8,128)S(1)}) fusion(f32[512,256]{1,0:T(8,128)S(1)} %get-tuple-element.328, f32[1,512,256]{2,1,0:T(8,128)S(1)} %get-tuple-element.318, f32[1,512,512]{2,1,0:T(8,128)S(1)} %get-tuple-element.327), kind=kOutput, calls=%fused_computation.27.clone.1 | convolution fusion | flops 805699584 | bytes 2621444 | tf_op jit(solution)/shard_map/while/body/...ij,...jk->...ik/dot_general | solution.py:12
  41.7 0.7 fusion.216
  43.5 1.1 %fusion.171 = (f32[1,256,256]{2,1,0:T(8,128)S(1)}, f32[1,256,256]{2,1,0:T(8,128)S(1)}) fusion(f32[1,512,256]{2,1,0:T(8,128)} %collective-permute-done.1, f32[256]{0:T(256)S(1)} %mul.733), kind=kLoop, calls=%fused_computation.347 | loop fusion | flops 196608 | bytes 1049600 | tf_op jit(solution)/shard_map/slice | solution.py:31
  45.4 1.0 %convolution_bitcast_fusion.2 = f32[1,512,256]{2,1,0:T(8,128)S(1)} fusion(f32[1,256,256]{1,2,0:T(8,128)S(1)} %get-tuple-element.120, f32[1,256,256]{1,2,0:T(8,128)S(1)} %get-tuple-element.119, f32[1,256,256]{1,2,0:T(8,128)S(1)} %get-tuple-element.118, f32[1,256,256]{2,1,0:T(8,128)S(1)} %bitcast_negate_fusion, f32[1,256,256]{2,1,0:T(8,128)S(1)} %bitcast.388), kind=kOutput, calls=%fused_computation.56 | convolution fusion | flops 403570688 | bytes 1835008 | tf_op jit(solution)/shard_map/...ij,...jk->...ik/dot_general | solution.py:12
  46.6 38.7 %all_to_all.5 = f32[16,1,4,16,256]{4,3,2,1,0:T(8,128)S(1)} all-to-all(f32[16,1,4,16,256]{4,3,2,1,0:T(8,128)S(1)} %maximum_bitcast_fusion.22), channel_id=1, replica_groups=mesh['groups'=2,'energy'=8,'space'=2] {'energy','space'}, dimensions={0} | all-to-all | bytes 2097152 | tf_op jit(solution)/shard_map/all_to_all | solution.py:131
  86.1 0.8 copy.40
  (116 shorter events, 21.6 us)
Async XLA Ops:
  0.0 0.7 copy-start.3
  0.1 0.7 copy-start.2
  14.2 1.0 %copy-start.1 = (f32[512,256]{1,0:T(8,128)S(1)}, f32[512,256]{1,0:T(8,128)}, u32[]{:S(2)}) copy-start(f32[512,256]{1,0:T(8,128)} %select_subtract_fusion.5) | copy-start | bytes 1572868
  16.3 3.3 %copy-start = (f32[1,2,256,256]{3,2,1,0:T(8,128)S(1)}, f32[1,2,256,256]{3,2,1,0:T(8,128)}, u32[]{:S(2)}) copy-start(f32[1,2,256,256]{3,2,1,0:T(8,128)} %param.10) | copy-start | bytes 1572868
  21.2 1.1 %copy-start.4 = (f32[1,1,256]{2,1,0:T(1,128)S(1)}, f32[1,1,256]{2,1,0:T(1,128)}, u32[]{:S(2)}) copy-start(f32[1,1,256]{2,1,0:T(1,128)} %param.13) | copy-start | bytes 3076
  22.2 4.2 %collective-permute-start = (f32[1,512,256]{2,1,0:T(8,128)S(1)}, f32[1,512,256]{2,1,0:T(8,128)S(1)}, u32[]{:S(2)}, u32[]{:S(2)}) collective-permute-start(f32[1,512,256]{2,1,0:T(8,128)S(1)} %convolution_bitcast_fusion.8), channel_id=1, source_target_pairs={{0,1},{1,0},{2,3},{3,2},{4,5},{5,4},{6,7},{7,6},{8,9},{9,8},{10,11... | collective-permute-start | bytes 1572872 | tf_op jit(solution)/shard_map/ppermute | solution.py:8
  26.0 17.6 %collective-permute-start.1 = (f32[1,512,256]{2,1,0:T(8,128)}, f32[1,512,256]{2,1,0:T(8,128)}, u32[]{:S(2)}, u32[]{:S(2)}) collective-permute-start(f32[1,512,256]{2,1,0:T(8,128)} %convolution_bitcast_fusion.4), channel_id=1, source_target_pairs={{0,1},{1,0},{2,3},{3,2},{4,5},{5,4},{6,7},{7,6},{8,9},{9,8},{10,11... | collective-permute-start | bytes 1572872 | tf_op jit(solution)/shard_map/ppermute | solution.py:8

commit v5 on v0

--- a/solution.py
+++ b/solution.py
@@ -44,18 +44,20 @@
     fourth = dot(embed(*split(square)), square, high)
     fourth_re, fourth_im = split(fourth)
     rows = jnp.sum(jnp.abs(fourth_re) + jnp.abs(fourth_im), axis=-1)
-    beta = jnp.sqrt(jnp.sqrt(jnp.max(rows, axis=-1))) * 1.01 + 1e-30
-    beta = beta[..., None, None]
+    largest = jnp.max(rows, axis=-1, keepdims=True)[..., None, :]
+    largest = jnp.broadcast_to(largest, largest.shape[:-1] + (2 * order,))
+    beta = jnp.sqrt(jnp.sqrt(largest)) * 1.01 + 1e-30
     lower = 0.25 / beta
     alpha = 2.0 / (lower + 1.0)
-    first_step = 2.0 * eye - (alpha / beta) * gram
-    approx = jnp.einsum("...ji,...jk->...ik", matrix, first_step, precision=high) * (alpha / beta)
+    scale = (alpha / beta)[..., :order]
+    first_step = 2.0 * eye - scale * gram
+    approx = jnp.einsum("...ji,...jk->...ik", matrix, first_step, precision=high) * scale
     ratio = (1.0 - lower) / (1.0 + lower)
     lower = 1.0 - ratio * ratio
     for _ in range(5):
         alpha = 2.0 / (lower + 1.0)
         product = dot(matrix, approx, high)
-        approx = dot(alpha * embed(*split(approx)), 2.0 * eye - alpha * product, high)
+        approx = dot(alpha * embed(*split(approx)), 2.0 * eye - alpha[..., :order] * product, high)
         ratio = (1.0 - lower) / (1.0 + lower)
         lower = 1.0 - ratio * ratio
 

time: 82.2 us -> 85.4 us (1.039)
  other arithmetic: 9.38 us -> 11.6 us
  local copies, waits for them, and re-layouts: 2.38 us -> 3.47 us
    neg x23, other arithmetic: 3.15 us -> 5.44 us  [embed(): top = jnp.concatenate([real, -imag], axis=-1)]
    unnamed x24 -> x34, local copies, waits for them, and re-layouts: 0.79 us -> 1.88 us
  transfers between devices with their start and end apart: 2 -> 2, of which waited for: 0 -> 0; matrix products, arithmetic and copies ran while one was open for 22% -> 23% of each run, Pallas kernels for 0% -> 0%
where the time goes in v5:
time: 85.4 us; the launch traced here: 83.8 us
  blocking collectives  32.4 us (38%)
  matrix products  30.9 us (36%)
  other arithmetic  11.6 us (14%)
  local copies, waits for them, and re-layouts  3.47 us (4%)
  between operations  3.34 us (4%)
  loops' own time  1.54 us (2%)
    all_to_all x1, blocking collectives, body(): lax.all_to_all(paired, ('energy', 'space'), split_axis=0, concat_axis=0,...  32.4 us
    dot_general x35, matrix products, dot(): return jnp.einsum('...ij,...jk->...ik', left, right, precision=precision)  28.4 us
    neg x23, other arithmetic, embed(): top = jnp.concatenate([real, -imag], axis=-1)  5.44 us
    concatenate x12, other arithmetic, embed(): return jnp.concatenate([top, bottom], axis=-2)  2.26 us
    unnamed x34, local copies, waits for them, and re-layouts  1.88 us
  transfers between devices with their start and end apart: 2, of which 0 were waited for; matrix products, arithmetic and copies ran while one was open for 23% of the time, Pallas kernels for 0%

profile of v5, /device:TPU:1, one launch (start us, length us, event | category | flops | bytes accessed | tf_op | source)
XLA Modules:
  0.0 83.8 jit_solution(1304189984908631230)
XLA Ops:
  0.7 1.2 %fusion.177 = (f32[1,256,256]{2,1,0:T(8,128)S(1)}, f32[1,256,256]{2,1,0:T(8,128)S(1)}, f32[1,256,256]{2,1,0:T(8,128)S(1)}) fusion(f32[1,2,256,256]{3,2,1,0:T(8,128)} %param.9, f32[256]{0:T(256)S(1)} %bitcast.376, f32[256]{0:T(256)S(1)} %bitcast.380, f32[]{:T(128)S(6)} %add.205), kind=kLoop, calls=%fused_computation.353 | loop fusion | flops 524288 | bytes 1312772 | tf_op jit(solution)/shard_map/neg | solution.py:20
  10.7 0.8 slice_negate_fusion.15
  13.2 0.8 slice_negate_fusion.14
  14.1 1.4 %select_subtract_fusion.6 = f32[512,256]{0,1:T(8,128)} fusion(f32[512,256]{0,1:T(8,128)S(1)} %fusion.42, pred[256,256]{0,1:T(32,128)(4,1)S(1)} %iota_compare_fusion, f32[]{:T(128)S(6)} %div.216, f32[1,256,256]{2,1,0:T(8,128)S(1)} %get-tuple-element.215, f32[1,256,256]{2,1,0:T(8,128)S(1)} %get-tuple-element.130, f32[1,256,256]{2,1,0:T(8,128)S(1)} %get-tuple-element.129), kind=kOutput, calls=%fused_computation.36 | convolution fusion | flops 403832832 | bytes 1900548 | tf_op jit(solution)/shard_map/...ij,...jk->...ik/dot_general | solution.py:12
  15.7 1.2 %maximum_bitcast_fusion.33 = (f32[256,512]{0,1:T(8,128)S(1)}, f32[256,512]{0,1:T(8,128)S(1)}) fusion(f32[1,256,256]{1,2,0:T(8,128)S(1)} %get-tuple-element.191, f32[1,256,256]{1,2,0:T(8,128)} %get-tuple-element.193, f32[1,256,256]{1,2,0:T(8,128)S(1)} %get-tuple-element.192), kind=kLoop, calls=%fused_computation.194 | loop fusion | flops 262144 | bytes 1835008 | tf_op jit(solution)/shard_map/concatenate | solution.py:22
  16.9 1.0 %convolution_bitcast_fusion.10 = f32[1,512,256]{2,1,0:T(8,128)S(1)} fusion(f32[512,256]{0,1:T(8,128)S(1)} %copy-done.6, f32[256,512]{0,1:T(8,128)S(1)} %get-tuple-element.229, f32[256,512]{0,1:T(8,128)S(1)} %get-tuple-element.228, f32[]{:T(128)S(6)} %div.216), kind=kOutput, calls=%fused_computation.62 | convolution fusion | flops 403177472 | bytes 2097156 | tf_op jit(solution)/shard_map/...ij,...jk->...ik/dot_general | solution.py:12
  17.9 3.3 %while.24 = (f32[1,512,256]{2,1,0:T(8,128)S(1)}, f32[]{:T(128)}, s32[]{:T(128)}, f32[1,512,512]{2,1,0:T(8,128)S(1)}, f32[512,256]{1,0:T(8,128)S(1)}, /*index=5*/s32[]{:T(128)}) while((f32[1,512,256]{2,1,0:T(8,128)S(1)}, f32[]{:T(128)}, s32[]{:T(128)}, f32[1,512,512]{2,1,0:T(8,128)S(1)}, f32[512,256]{1,0:T(8,128)S(1)}, ...), condition=%wide.region_4.5_spmd, body=%wide.region_2.4_spmd.sunk | while | flops 1209335808 | bytes 6291549 | solution.py:74
  17.9 1.6 %multiply_reduce_fusion.4 = (f32[]{:T(128)}, f32[512,256]{1,0:T(8,128)S(1)}) fusion(f32[512,256]{1,0:T(8,128)S(1)} %get-tuple-element.340, f32[1,512,256]{2,1,0:T(8,128)S(1)} %get-tuple-element.330, f32[1,512,512]{2,1,0:T(8,128)S(1)} %get-tuple-element.339), kind=kOutput, calls=%fused_computation.12.clone.1 | convolution fusion | flops 805699584 | bytes 2621444 | tf_op jit(solution)/shard_map/while/body/...ij,...jk->...ik/dot_general | solution.py:12
  19.6 0.7 fusion.218
  21.6 1.0 %convolution_bitcast_fusion.9 = f32[1,512,256]{1,2,0:T(8,128)S(1)} fusion(f32[256,256]{1,0:T(8,128)S(1)} %get-tuple-element.212, f32[256,256]{1,0:T(8,128)S(1)} %get-tuple-element.128, f32[256,256]{1,0:T(8,128)S(1)} %neg.110, f32[1,512,256]{2,1,0:T(8,128)S(1)} %get-tuple-element.59), kind=kOutput, calls=%fused_computation.61 | convolution fusion | flops 403439616 | bytes 1835008 | tf_op jit(solution)/shard_map/...ij,...jk->...ik/dot_general | solution.py:12
  22.8 1.0 %convolution_bitcast_fusion.8 = f32[1,512,256]{2,1,0:T(8,128)S(1)} fusion(f32[1,256,256]{1,2,0:T(8,128)S(1)} %get-tuple-element.190, f32[1,256,256]{1,2,0:T(8,128)S(1)} %get-tuple-element.189, f32[1,256,256]{1,2,0:T(8,128)S(1)} %get-tuple-element.188, f32[256,256]{0,1:T(8,128)S(1)} %get-tuple-element.127, f32[256,256]{0,1:T(8,128)S(1)} %bitcast.374), kind=kOutput, calls=%fused_computation.60 | convolution fusion | flops 403570688 | bytes 1835008 | tf_op jit(solution)/shard_map/...ij,...jk->...ik/dot_general | solution.py:12
  24.6 1.0 %convolution_bitcast_fusion.5 = f32[1,512,256]{1,2,0:T(8,128)S(1)} fusion(f32[512,256]{1,0:T(8,128)S(1)} %fusion.86, f32[256,256]{1,0:T(8,128)S(1)} %get-tuple-element.212, f32[256,256]{1,0:T(8,128)S(1)} %get-tuple-element.128, f32[256,256]{1,0:T(8,128)S(1)} %neg.110), kind=kOutput, calls=%fused_computation.57 | convolution fusion | flops 403439616 | bytes 1835008 | tf_op jit(solution)/shard_map/...ij,...jk->...ik/dot_general | solution.py:12
  25.7 1.8 %convolution_bitcast_fusion.4 = f32[1,512,256]{2,1,0:T(8,128)} fusion(f32[1,256,256]{1,2,0:T(8,128)S(1)} %get-tuple-element.155, f32[1,256,256]{1,2,0:T(8,128)S(1)} %get-tuple-element.154, f32[1,256,256]{1,2,0:T(8,128)S(1)} %get-tuple-element.153, f32[256,256]{0,1:T(8,128)S(1)} %get-tuple-element.127, f32[256,256]{0,1:T(8,128)S(1)} %bitcast.375), kind=kOutput, calls=%fused_computation.56 | convolution fusion | flops 403570688 | bytes 1835008 | tf_op jit(solution)/shard_map/...ij,...jk->...ik/dot_general | solution.py:12
  36.7 0.8 %fusion.72 = f32[512,256]{0,1:T(8,128)S(1)} fusion(f32[512,256]{0,1:T(8,128)S(1)} %select_subtract_fusion.2, f32[256,512]{0,1:T(8,128)S(1)} %get-tuple-element.221, f32[256,512]{0,1:T(8,128)S(1)} %get-tuple-element.220, f32[]{:T(128)S(6)} %div.230), kind=kOutput, calls=%fused_computation.133 | convolution fusion | flops 403177472 | bytes 2097156 | tf_op jit(solution)/shard_map/...ij,...jk->...ik/dot_general | solution.py:12
  37.5 0.9 %slice_negate_fusion.6 = (f32[1,256,256]{1,2,0:T(8,128)S(1)}, f32[1,256,256]{1,2,0:T(8,128)}, f32[1,256,256]{1,2,0:T(8,128)}) fusion(f32[1,512,256]{1,2,0:T(8,128)S(1)} %bitcast.356), kind=kLoop, calls=%fused_computation.335 | loop fusion | flops 65536 | bytes 1310720 | tf_op jit(solution)/shard_map/neg | solution.py:20
  40.2 0.9 %slice_negate_fusion.5 = (f32[1,256,256]{1,2,0:T(8,128)S(1)}, f32[1,256,256]{1,2,0:T(8,128)}, f32[1,256,256]{1,2,0:T(8,128)}) fusion(f32[1,512,256]{1,2,0:T(8,128)S(1)} %bitcast.355), kind=kLoop, calls=%fused_computation.334 | loop fusion | flops 65536 | bytes 1310720 | tf_op jit(solution)/shard_map/neg | solution.py:20
  42.3 1.0 %convolution_bitcast_fusion.6 = f32[1,512,256]{2,1,0:T(8,128)S(1)} fusion(f32[512,256]{0,1:T(8,128)S(1)} %select_subtract_fusion, f32[256,512]{0,1:T(8,128)S(1)} %get-tuple-element.217, f32[256,512]{0,1:T(8,128)S(1)} %get-tuple-element.216, f32[]{:T(128)S(6)} %div.228), kind=kOutput, calls=%fused_computation.58 | convolution fusion | flops 403177472 | bytes 2097156 | tf_op jit(solution)/shard_map/...ij,...jk->...ik/dot_general | solution.py:12
  43.3 3.0 %while.25 = (f32[1,512,256]{2,1,0:T(8,128)S(1)}, f32[]{:T(128)}, s32[]{:T(128)}, f32[1,512,512]{2,1,0:T(8,128)S(1)}, f32[512,256]{1,0:T(8,128)S(1)}, /*index=5*/s32[]{:T(128)}) while((f32[1,512,256]{2,1,0:T(8,128)S(1)}, f32[]{:T(128)}, s32[]{:T(128)}, f32[1,512,512]{2,1,0:T(8,128)S(1)}, f32[512,256]{1,0:T(8,128)S(1)}, ...), condition=%wide.region_9.0_spmd, body=%wide.region_7.0_spmd.sunk | while | flops 1209335808 | bytes 6291549 | solution.py:74
  43.3 1.6 %multiply_reduce_fusion.5 = (f32[]{:T(128)}, f32[512,256]{1,0:T(8,128)S(1)}) fusion(f32[512,256]{1,0:T(8,128)S(1)} %get-tuple-element.358, f32[1,512,256]{2,1,0:T(8,128)S(1)} %get-tuple-element.348, f32[1,512,512]{2,1,0:T(8,128)S(1)} %get-tuple-element.357), kind=kOutput, calls=%fused_computation.27.clone.1 | convolution fusion | flops 805699584 | bytes 2621444 | tf_op jit(solution)/shard_map/while/body/...ij,...jk->...ik/dot_general | solution.py:12
  44.9 0.7 fusion.220
  46.7 1.1 %fusion.178 = (f32[1,256,256]{2,1,0:T(8,128)S(1)}, f32[1,256,256]{2,1,0:T(8,128)S(1)}) fusion(f32[1,512,256]{2,1,0:T(8,128)} %collective-permute-done.1, f32[256]{0:T(256)S(1)} %mul.785), kind=kLoop, calls=%fused_computation.354 | loop fusion | flops 196608 | bytes 1049600 | tf_op jit(solution)/shard_map/slice | solution.py:31
  48.5 1.0 %convolution_bitcast_fusion.2 = f32[1,512,256]{2,1,0:T(8,128)S(1)} fusion(f32[1,256,256]{1,2,0:T(8,128)S(1)} %get-tuple-element.150, f32[1,256,256]{1,2,0:T(8,128)S(1)} %get-tuple-element.149, f32[1,256,256]{1,2,0:T(8,128)S(1)} %get-tuple-element.148, f32[1,256,256]{2,1,0:T(8,128)S(1)} %bitcast_negate_fusion, f32[1,256,256]{2,1,0:T(8,128)S(1)} %bitcast.365), kind=kOutput, calls=%fused_computation.54 | convolution fusion | flops 403570688 | bytes 1835008 | tf_op jit(solution)/shard_map/...ij,...jk->...ik/dot_general | solution.py:12
  49.7 32.4 %all_to_all.5 = f32[16,1,4,16,256]{4,3,2,1,0:T(8,128)S(1)} all-to-all(f32[16,1,4,16,256]{4,3,2,1,0:T(8,128)S(1)} %maximum_bitcast_fusion.22), channel_id=1, replica_groups=mesh['groups'=2,'energy'=8,'space'=2] {'energy','space'}, dimensions={0} | all-to-all | bytes 2097152 | tf_op jit(solution)/shard_map/all_to_all | solution.py:131
  82.9 0.8 %copy.56 = f32[8,2,2,16,256]{4,3,2,1,0:T(8,128)} copy(f32[8,2,2,16,256]{4,3,1,2,0:T(8,128)S(1)} %pad_maximum_fusion.1) | data formatting | bytes 1048576 | tf_op jit(solution)/shard_map/stack | solution.py:148
  (125 shorter events, 24.1 us)
Async XLA Ops:
  0.0 0.7 copy-start.8
  0.1 0.7 copy-start.7
  11.5 1.0 %copy-start.3 = (f32[1,256,256]{1,2,0:T(8,128)S(1)}, f32[1,256,256]{1,2,0:T(8,128)}, u32[]{:S(2)}) copy-start(f32[1,256,256]{1,2,0:T(8,128)} %get-tuple-element.196) | copy-start | bytes 786436
  15.7 1.2 %copy-start.6 = (f32[512,256]{0,1:T(8,128)S(1)}, f32[512,256]{0,1:T(8,128)}, u32[]{:S(2)}) copy-start(f32[512,256]{0,1:T(8,128)} %select_subtract_fusion.6) | copy-start | bytes 1572868
  17.9 3.3 %copy-start = (f32[1,2,256,256]{3,2,1,0:T(8,128)S(1)}, f32[1,2,256,256]{3,2,1,0:T(8,128)}, u32[]{:S(2)}) copy-start(f32[1,2,256,256]{3,2,1,0:T(8,128)} %param.10) | copy-start | bytes 1572868
  22.8 1.1 %copy-start.9 = (f32[1,1,256]{2,1,0:T(1,128)S(1)}, f32[1,1,256]{2,1,0:T(1,128)}, u32[]{:S(2)}) copy-start(f32[1,1,256]{2,1,0:T(1,128)} %param.13) | copy-start | bytes 3076
  23.8 4.2 %collective-permute-start = (f32[1,512,256]{2,1,0:T(8,128)S(1)}, f32[1,512,256]{2,1,0:T(8,128)S(1)}, u32[]{:S(2)}, u32[]{:S(2)}) collective-permute-start(f32[1,512,256]{2,1,0:T(8,128)S(1)} %convolution_bitcast_fusion.8), channel_id=1, source_target_pairs={{0,1},{1,0},{2,3},{3,2},{4,5},{5,4},{6,7},{7,6},{8,9},{9,8},{10,11... | collective-permute-start | bytes 1572872 | tf_op jit(solution)/shard_map/ppermute | solution.py:8
  27.5 19.1 %collective-permute-start.1 = (f32[1,512,256]{2,1,0:T(8,128)}, f32[1,512,256]{2,1,0:T(8,128)}, u32[]{:S(2)}, u32[]{:S(2)}) collective-permute-start(f32[1,512,256]{2,1,0:T(8,128)} %convolution_bitcast_fusion.4), channel_id=1, source_target_pairs={{0,1},{1,0},{2,3},{3,2},{4,5},{5,4},{6,7},{7,6},{8,9},{9,8},{10,11... | collective-permute-start | bytes 1572872 | tf_op jit(solution)/shard_map/ppermute | solution.py:8
  38.4 1.0 %copy-start.4 = (f32[1,256,256]{1,2,0:T(8,128)S(1)}, f32[1,256,256]{1,2,0:T(8,128)}, u32[]{:S(2)}) copy-start(f32[1,256,256]{1,2,0:T(8,128)} %get-tuple-element.168) | copy-start | bytes 786436
  38.5 1.0 %copy-start.5 = (f32[1,256,256]{1,2,0:T(8,128)S(1)}, f32[1,256,256]{1,2,0:T(8,128)}, u32[]{:S(2)}) copy-start(f32[1,256,256]{1,2,0:T(8,128)} %get-tuple-element.169) | copy-start | bytes 786436
  41.1 1.0 %copy-start.1 = (f32[1,256,256]{1,2,0:T(8,128)S(1)}, f32[1,256,256]{1,2,0:T(8,128)}, u32[]{:S(2)}) copy-start(f32[1,256,256]{1,2,0:T(8,128)} %get-tuple-element.165) | copy-start | bytes 786436
  41.1 1.0 %copy-start.2 = (f32[1,256,256]{1,2,0:T(8,128)S(1)}, f32[1,256,256]{1,2,0:T(8,128)}, u32[]{:S(2)}) copy-start(f32[1,256,256]{1,2,0:T(8,128)} %get-tuple-element.166) | copy-start | bytes 786436

commit v6 on v0

--- a/solution.py
+++ b/solution.py
@@ -61,12 +61,12 @@
 
     def keep_going(state):
         _, residual, count = state
-        return (residual > 2e-3) & (count < 40)
+        return (residual > 4e-6) & (count < 40)
 
     def newton(state):
         approx, _, count = state
         rest = eye - dot(matrix, approx)
-        residual = jnp.sqrt(jnp.max(jnp.sum(rest * rest, axis=(-1, -2))))
+        residual = jnp.max(jnp.sum(rest * rest, axis=(-1, -2)))
         return approx + dot(embed(*split(approx)), rest, high), residual, count + 1
 
     approx, _, _ = lax.while_loop(

time: 82.2 us -> 80.5 us (0.979); the launches traced: 80.6 us -> 80.3 us
  no operation moved by 1% of the time
where the time goes in v6:
time: 80.5 us; the launch traced here: 80.3 us
  blocking collectives  32.4 us (40%)
  matrix products  30.8 us (38%)
  other arithmetic  9.38 us (12%)
  between operations  3.41 us (4%)
  local copies, waits for them, and re-layouts  2.38 us (3%)
  loops' own time  1.36 us (2%)
    all_to_all x1, blocking collectives, body(): lax.all_to_all(paired, ('energy', 'space'), split_axis=0, concat_axis=0,...  32.4 us
    dot_general x35, matrix products, dot(): return jnp.einsum('...ij,...jk->...ik', left, right, precision=precision)  28.3 us
    neg x23, other arithmetic, embed(): top = jnp.concatenate([real, -imag], axis=-1)  3.15 us
    concatenate x12, other arithmetic, embed(): return jnp.concatenate([top, bottom], axis=-2)  2.28 us
  transfers between devices with their start and end apart: 2, of which 0 were waited for; matrix products, arithmetic and copies ran while one was open for 22% of the time, Pallas kernels for 0%

profile of v6, /device:TPU:1, one launch (start us, length us, event | category | flops | bytes accessed | tf_op | source)
XLA Modules:
  0.0 80.3 jit_solution(8503333750586488725)
XLA Ops:
  0.1 0.7 copy-done.3
  0.7 1.2 %fusion.177 = (f32[1,256,256]{2,1,0:T(8,128)S(1)}, f32[1,256,256]{2,1,0:T(8,128)S(1)}, f32[1,256,256]{2,1,0:T(8,128)S(1)}) fusion(f32[1,2,256,256]{3,2,1,0:T(8,128)} %param.9, f32[256]{0:T(256)S(1)} %bitcast.390, f32[256]{0:T(256)S(1)} %bitcast.394, f32[]{:T(128)S(6)} %add.151), kind=kLoop, calls=%fused_computation.353 | loop fusion | flops 524288 | bytes 1312772 | tf_op jit(solution)/shard_map/neg | solution.py:20
  5.8 0.6 convolution_multiply_fusion.11
  12.2 0.8 slice_negate_fusion.14
  13.0 1.4 %select_subtract_fusion.6 = f32[512,256]{0,1:T(8,128)} fusion(f32[512,256]{0,1:T(8,128)S(1)} %fusion.42, pred[256,256]{0,1:T(32,128)(4,1)S(1)} %iota_compare_fusion, f32[]{:T(128)} %bitcast.21, f32[1,256,256]{2,1,0:T(8,128)S(1)} %get-tuple-element.215, f32[1,256,256]{2,1,0:T(8,128)S(1)} %get-tuple-element.130, f32[1,256,256]{2,1,0:T(8,128)S(1)} %get-tuple-element.129), kind=kOutput, calls=%fused_computation.36 | convolution fusion | flops 403832832 | bytes 1900548 | tf_op jit(solution)/shard_map/...ij,...jk->...ik/dot_general | solution.py:12
  14.7 1.2 %maximum_bitcast_fusion.33 = (f32[256,512]{0,1:T(8,128)S(1)}, f32[256,512]{0,1:T(8,128)S(1)}) fusion(f32[1,256,256]{1,2,0:T(8,128)S(1)} %get-tuple-element.191, f32[1,256,256]{1,2,0:T(8,128)} %get-tuple-element.193, f32[1,256,256]{1,2,0:T(8,128)S(1)} %get-tuple-element.192), kind=kLoop, calls=%fused_computation.194 | loop fusion | flops 262144 | bytes 1835008 | tf_op jit(solution)/shard_map/concatenate | solution.py:22
  15.9 1.0 %convolution_bitcast_fusion.10 = f32[1,512,256]{2,1,0:T(8,128)S(1)} fusion(f32[512,256]{0,1:T(8,128)S(1)} %copy-done.1, f32[256,512]{0,1:T(8,128)S(1)} %get-tuple-element.229, f32[256,512]{0,1:T(8,128)S(1)} %get-tuple-element.228, f32[]{:T(128)} %bitcast.21), kind=kOutput, calls=%fused_computation.62 | convolution fusion | flops 403177472 | bytes 2097156 | tf_op jit(solution)/shard_map/...ij,...jk->...ik/dot_general | solution.py:12
  16.9 3.1 %while.24 = (f32[1,512,256]{2,1,0:T(8,128)S(1)}, f32[]{:T(128)}, s32[]{:T(128)}, f32[1,512,512]{2,1,0:T(8,128)S(1)}, f32[512,256]{1,0:T(8,128)S(1)}, /*index=5*/s32[]{:T(128)}) while((f32[1,512,256]{2,1,0:T(8,128)S(1)}, f32[]{:T(128)}, s32[]{:T(128)}, f32[1,512,512]{2,1,0:T(8,128)S(1)}, f32[512,256]{1,0:T(8,128)S(1)}, ...), condition=%wide.region_4.5_spmd, body=%wide.region_2.4_spmd.sunk | while | flops 1209335808 | bytes 6291541 | solution.py:72
  16.9 1.6 %multiply_reduce_fusion.4 = (f32[]{:T(128)}, f32[512,256]{1,0:T(8,128)S(1)}) fusion(f32[512,256]{1,0:T(8,128)S(1)} %get-tuple-element.340, f32[1,512,256]{2,1,0:T(8,128)S(1)} %get-tuple-element.330, f32[1,512,512]{2,1,0:T(8,128)S(1)} %get-tuple-element.339), kind=kOutput, calls=%fused_computation.12.clone.1 | convolution fusion | flops 805699584 | bytes 2621444 | tf_op jit(solution)/shard_map/while/body/...ij,...jk->...ik/dot_general | solution.py:12
  18.5 0.7 fusion.218
  20.5 1.0 %convolution_bitcast_fusion.9 = f32[1,512,256]{1,2,0:T(8,128)S(1)} fusion(f32[256,256]{1,0:T(8,128)S(1)} %get-tuple-element.212, f32[256,256]{1,0:T(8,128)S(1)} %get-tuple-element.128, f32[256,256]{1,0:T(8,128)S(1)} %neg.110, f32[1,512,256]{2,1,0:T(8,128)S(1)} %get-tuple-element.59), kind=kOutput, calls=%fused_computation.61 | convolution fusion | flops 403439616 | bytes 1835008 | tf_op jit(solution)/shard_map/...ij,...jk->...ik/dot_general | solution.py:12
  21.6 1.0 %convolution_bitcast_fusion.8 = f32[1,512,256]{2,1,0:T(8,128)S(1)} fusion(f32[1,256,256]{1,2,0:T(8,128)S(1)} %get-tuple-element.190, f32[1,256,256]{1,2,0:T(8,128)S(1)} %get-tuple-element.189, f32[1,256,256]{1,2,0:T(8,128)S(1)} %get-tuple-element.188, f32[256,256]{0,1:T(8,128)S(1)} %get-tuple-element.127, f32[256,256]{0,1:T(8,128)S(1)} %bitcast.388), kind=kOutput, calls=%fused_computation.60 | convolution fusion | flops 403570688 | bytes 1835008 | tf_op jit(solution)/shard_map/...ij,...jk->...ik/dot_general | solution.py:12
  23.4 1.0 %convolution_bitcast_fusion.5 = f32[1,512,256]{1,2,0:T(8,128)S(1)} fusion(f32[512,256]{1,0:T(8,128)S(1)} %fusion.86, f32[256,256]{1,0:T(8,128)S(1)} %get-tuple-element.212, f32[256,256]{1,0:T(8,128)S(1)} %get-tuple-element.128, f32[256,256]{1,0:T(8,128)S(1)} %neg.110), kind=kOutput, calls=%fused_computation.57 | convolution fusion | flops 403439616 | bytes 1835008 | tf_op jit(solution)/shard_map/...ij,...jk->...ik/dot_general | solution.py:12
  24.5 1.8 %convolution_bitcast_fusion.4 = f32[1,512,256]{2,1,0:T(8,128)} fusion(f32[1,256,256]{1,2,0:T(8,128)S(1)} %get-tuple-element.155, f32[1,256,256]{1,2,0:T(8,128)S(1)} %get-tuple-element.154, f32[1,256,256]{1,2,0:T(8,128)S(1)} %get-tuple-element.153, f32[256,256]{0,1:T(8,128)S(1)} %get-tuple-element.127, f32[256,256]{0,1:T(8,128)S(1)} %bitcast.389), kind=kOutput, calls=%fused_computation.56 | convolution fusion | flops 403570688 | bytes 1835008 | tf_op jit(solution)/shard_map/...ij,...jk->...ik/dot_general | solution.py:12
  29.6 0.7 reduce_max.21
  35.7 0.8 %fusion.72 = f32[512,256]{0,1:T(8,128)S(1)} fusion(f32[512,256]{0,1:T(8,128)S(1)} %select_subtract_fusion.2, f32[256,512]{0,1:T(8,128)S(1)} %get-tuple-element.221, f32[256,512]{0,1:T(8,128)S(1)} %get-tuple-element.220, f32[]{:T(128)} %bitcast.66), kind=kOutput, calls=%fused_computation.133 | convolution fusion | flops 403177472 | bytes 2097156 | tf_op jit(solution)/shard_map/...ij,...jk->...ik/dot_general | solution.py:12
  38.8 1.0 %convolution_bitcast_fusion.6 = f32[1,512,256]{2,1,0:T(8,128)S(1)} fusion(f32[512,256]{0,1:T(8,128)S(1)} %select_subtract_fusion, f32[256,512]{0,1:T(8,128)S(1)} %get-tuple-element.217, f32[256,512]{0,1:T(8,128)S(1)} %get-tuple-element.216, f32[]{:T(128)} %bitcast.64), kind=kOutput, calls=%fused_computation.58 | convolution fusion | flops 403177472 | bytes 2097156 | tf_op jit(solution)/shard_map/...ij,...jk->...ik/dot_general | solution.py:12
  39.8 3.0 %while.25 = (f32[1,512,256]{2,1,0:T(8,128)S(1)}, f32[]{:T(128)}, s32[]{:T(128)}, f32[1,512,512]{2,1,0:T(8,128)S(1)}, f32[512,256]{1,0:T(8,128)S(1)}, /*index=5*/s32[]{:T(128)}) while((f32[1,512,256]{2,1,0:T(8,128)S(1)}, f32[]{:T(128)}, s32[]{:T(128)}, f32[1,512,512]{2,1,0:T(8,128)S(1)}, f32[512,256]{1,0:T(8,128)S(1)}, ...), condition=%wide.region_9.0_spmd, body=%wide.region_7.0_spmd.sunk | while | flops 1209335808 | bytes 6291541 | solution.py:72
  39.9 1.6 %multiply_reduce_fusion.5 = (f32[]{:T(128)}, f32[512,256]{1,0:T(8,128)S(1)}) fusion(f32[512,256]{1,0:T(8,128)S(1)} %get-tuple-element.358, f32[1,512,256]{2,1,0:T(8,128)S(1)} %get-tuple-element.348, f32[1,512,512]{2,1,0:T(8,128)S(1)} %get-tuple-element.357), kind=kOutput, calls=%fused_computation.27.clone.1 | convolution fusion | flops 805699584 | bytes 2621444 | tf_op jit(solution)/shard_map/while/body/...ij,...jk->...ik/dot_general | solution.py:12
  41.5 0.7 fusion.220
  43.2 1.1 %fusion.178 = (f32[1,256,256]{2,1,0:T(8,128)S(1)}, f32[1,256,256]{2,1,0:T(8,128)S(1)}) fusion(f32[1,512,256]{2,1,0:T(8,128)} %collective-permute-done.1, f32[256]{0:T(256)S(1)} %mul.713), kind=kLoop, calls=%fused_computation.354 | loop fusion | flops 196608 | bytes 1049600 | tf_op jit(solution)/shard_map/slice | solution.py:31
  45.0 1.0 %convolution_bitcast_fusion.2 = f32[1,512,256]{2,1,0:T(8,128)S(1)} fusion(f32[1,256,256]{1,2,0:T(8,128)S(1)} %get-tuple-element.150, f32[1,256,256]{1,2,0:T(8,128)S(1)} %get-tuple-element.149, f32[1,256,256]{1,2,0:T(8,128)S(1)} %get-tuple-element.148, f32[1,256,256]{2,1,0:T(8,128)S(1)} %bitcast_negate_fusion, f32[1,256,256]{2,1,0:T(8,128)S(1)} %bitcast.379), kind=kOutput, calls=%fused_computation.54 | convolution fusion | flops 403570688 | bytes 1835008 | tf_op jit(solution)/shard_map/...ij,...jk->...ik/dot_general | solution.py:12
  46.3 32.4 %all_to_all.5 = f32[16,1,4,16,256]{4,3,2,1,0:T(8,128)S(1)} all-to-all(f32[16,1,4,16,256]{4,3,2,1,0:T(8,128)S(1)} %maximum_bitcast_fusion.22), channel_id=1, replica_groups=mesh['groups'=2,'energy'=8,'space'=2] {'energy','space'}, dimensions={0} | all-to-all | bytes 2097152 | tf_op jit(solution)/shard_map/all_to_all | solution.py:129
  79.4 0.8 %copy.56 = f32[8,2,2,16,256]{4,3,2,1,0:T(8,128)} copy(f32[8,2,2,16,256]{4,3,1,2,0:T(8,128)S(1)} %pad_maximum_fusion.1) | data formatting | bytes 1048576 | tf_op jit(solution)/shard_map/stack | solution.py:146
  (115 shorter events, 21.3 us)
Async XLA Ops:
  0.0 0.7 copy-start.3
  0.1 0.7 copy-start.2
  14.7 1.2 %copy-start.1 = (f32[512,256]{0,1:T(8,128)S(1)}, f32[512,256]{0,1:T(8,128)}, u32[]{:S(2)}) copy-start(f32[512,256]{0,1:T(8,128)} %select_subtract_fusion.6) | copy-start | bytes 1572868
  16.9 3.2 %copy-start = (f32[1,2,256,256]{3,2,1,0:T(8,128)S(1)}, f32[1,2,256,256]{3,2,1,0:T(8,128)}, u32[]{:S(2)}) copy-start(f32[1,2,256,256]{3,2,1,0:T(8,128)} %param.10) | copy-start | bytes 1572868
  21.6 1.1 %copy-start.4 = (f32[1,1,256]{2,1,0:T(1,128)S(1)}, f32[1,1,256]{2,1,0:T(1,128)}, u32[]{:S(2)}) copy-start(f32[1,1,256]{2,1,0:T(1,128)} %param.13) | copy-start | bytes 3076
  22.6 4.2 %collective-permute-start = (f32[1,512,256]{2,1,0:T(8,128)S(1)}, f32[1,512,256]{2,1,0:T(8,128)S(1)}, u32[]{:S(2)}, u32[]{:S(2)}) collective-permute-start(f32[1,512,256]{2,1,0:T(8,128)S(1)} %convolution_bitcast_fusion.8), channel_id=1, source_target_pairs={{0,1},{1,0},{2,3},{3,2},{4,5},{5,4},{6,7},{7,6},{8,9},{9,8},{10,11... | collective-permute-start | bytes 1572872 | tf_op jit(solution)/shard_map/ppermute | solution.py:8
  26.3 16.8 %collective-permute-start.1 = (f32[1,512,256]{2,1,0:T(8,128)}, f32[1,512,256]{2,1,0:T(8,128)}, u32[]{:S(2)}, u32[]{:S(2)}) collective-permute-start(f32[1,512,256]{2,1,0:T(8,128)} %convolution_bitcast_fusion.4), channel_id=1, source_target_pairs={{0,1},{1,0},{2,3},{3,2},{4,5},{5,4},{6,7},{7,6},{8,9},{9,8},{10,11... | collective-permute-start | bytes 1572872 | tf_op jit(solution)/shard_map/ppermute | solution.py:8
